TPU v7x, 256 devices: a whole 4x4x8 slice. The times are simulated.
256 devices in a mesh: tm: 8 (over y_lo, x), stn: 32 (over y_hi, z, core).
Axes of the slice: x: 4, y: 4 (y_hi: 2, y_lo: 2; y = y_hi * 2 + y_lo), z: 8, core: 2. Of those that a mesh axis runs over, the one named last changes fastest.
Arguments:
- voltages: bfloat16 [1024, 524288], P('stn', 'tm'), may hold values from -6 to 6
- gains: float32 [2, 1024, 256], P(None, 'stn'), may hold values from -4 to 4
Outputs:
- visibility: float32 [256, 2, 1024, 1024], P(('tm', 'stn'))
All inputs are finite; a program needn't handle non-finite values.
Results may differ from a plain program's by a relative error of at most 0.0038.
Values may be sent and summed in bfloat16 or wider, within the bound.
No kernel may reach another device: no remote copies, remote signals or barrier semaphores. Data moves between devices by JAX's collectives and lax.ppermute only.
A program may use at most 128 MiB of HBM per device.

v0:
```python
import jax
import jax.numpy as jnp
from jax import lax
from jax.sharding import PartitionSpec as P

CHANNELS = 4096
BAND_LOW = 1024
TAPS = 8


def passed_along(x, axis, by):
    devices = lax.axis_size(axis)
    pairs = [(i, i + by) for i in range(devices) if 0 <= i + by < devices]
    return lax.ppermute(x, axis, pairs)


def window_table(chans):
    frame_len = 2 * chans
    total_len = TAPS * frame_len
    positions = jnp.arange(total_len, dtype=jnp.float32)
    centred = (positions - (total_len - 1) / 2.0) / frame_len
    taper = jnp.sin(jnp.pi * (positions + 0.5) / total_len)
    shaped = jnp.sinc(centred) * taper * taper
    shaped = shaped / jnp.sqrt(jnp.sum(shaped * shaped))
    return shaped.reshape(TAPS, frame_len)


def band_tables(frame_len, band):
    sample_index = jnp.arange(frame_len, dtype=jnp.int32)[:, None]
    channel_index = (BAND_LOW + jnp.arange(band, dtype=jnp.int32))[None, :]
    phase = (sample_index * channel_index % frame_len).astype(jnp.float32)
    angles = 2.0 * jnp.pi * phase / frame_len
    return (jnp.cos(angles), jnp.sin(angles))


def band_spectra(windowed, cos_table, sin_table):
    highest = lax.Precision.HIGHEST
    real_part = jnp.einsum("ifm,mk->kif", windowed, cos_table, precision=highest)
    imag_part = -jnp.einsum("ifm,mk->kif", windowed, sin_table, precision=highest)
    return (real_part, imag_part)


def apply_taps(window, extended, frames):
    windowed = jnp.zeros((extended.shape[0], frames, extended.shape[2]), jnp.float32)
    for tap_index in range(TAPS):
        windowed = windowed + window[tap_index] * extended[
            :, tap_index : tap_index + frames, :
        ].astype(jnp.float32)
    return windowed


def operands(turned):
    stacked = jnp.concatenate([turned[0], turned[1]], axis=-1)
    flipped = jnp.concatenate([turned[1], -turned[0]], axis=-1)
    return (stacked, flipped)


def cross_power(stacked, flipped, total_frames):
    vis_real = jnp.einsum("cif,cjf->cij", stacked, stacked, preferred_element_type=jnp.float32)
    vis_imag = jnp.einsum("cif,cjf->cij", flipped, stacked, preferred_element_type=jnp.float32)
    return jnp.stack([vis_real, vis_imag], axis=1) / total_frames


def on_device(voltages, gains):
    in_dev, length = voltages.shape
    band = gains.shape[2]
    frame_len = 2 * CHANNELS
    frames = length // frame_len
    n_time = lax.axis_size("tm")
    n_station = lax.axis_size("stn")
    per_device = band // (n_time * n_station)
    all_inputs = in_dev * n_station
    history = TAPS - 1
    window = window_table(CHANNELS)
    cos_table, sin_table = band_tables(frame_len, band)
    framed = voltages.reshape(in_dev, frames, frame_len)
    before = passed_along(framed[:, frames - history :, :], "tm", 1)
    extended = jnp.concatenate([before, framed], axis=1)
    windowed = apply_taps(window, extended, frames)
    raw_real, raw_imag = band_spectra(windowed, cos_table, sin_table)
    gain_real = jnp.transpose(gains[0])[:, :, None]
    gain_imag = jnp.transpose(gains[1])[:, :, None]
    spec_real = gain_real * raw_real - gain_imag * raw_imag
    spec_imag = gain_real * raw_imag + gain_imag * raw_real
    spectra = jnp.stack([spec_real, spec_imag]).astype(jnp.bfloat16)
    blocks = spectra.reshape(2, n_time, n_station, per_device, in_dev, frames)
    turned = lax.all_to_all(
        lax.all_to_all(blocks, "tm", split_axis=1, concat_axis=5, tiled=True),
        "stn",
        split_axis=2,
        concat_axis=4,
        tiled=True,
    )
    turned = turned.reshape(2, per_device, all_inputs, n_time * frames)
    stacked, flipped = operands(turned)
    return cross_power(stacked, flipped, float(n_time * frames))


def solution(mesh):
    in_specs = (P("stn", "tm"), P(None, "stn", None))
    out_specs = P(("tm", "stn"), None, None, None)
    return jax.shard_map(
        on_device, mesh=mesh, in_specs=in_specs, out_specs=out_specs, check_vma=False
    )
```

profile of v0, /device:TPU:1, one launch (start us, length us, event | category | flops | bytes accessed | tf_op | source)
XLA Modules:
  0.0 223.4 jit_solution(14158245446705456912)
XLA Ops:
  0.0 0.0 copy-start.1
  0.0 2.5 %copy.34 = bf16[4,8,8,8192]{3,2,0,1:T(8,128)(2,1)S(1)} copy(bf16[4,8,8,8192]{3,2,1,0:T(8,128)(2,1)} %bitcast.57) | data formatting | bytes 8388608 | tf_op jit(solution)/shard_map/reshape | solution.py:76
  2.5 2.1 slice.94
  4.6 5.7 %collective-permute-start = (bf16[32,7,8192]{2,0,1:T(8,128)(2,1)}, bf16[32,7,8192]{2,0,1:T(8,128)(2,1)}, u32[]{:S(2)}, u32[]{:S(2)}) collective-permute-start(bf16[32,7,8192]{2,0,1:T(8,128)(2,1)} %slice.94), channel_id=1, source_target_pairs={{0,32},{32,64},{64,96},{96,128},{128,160},{160,192},{192,224},{1,3... | collective-permute-start | bytes 11010056 | tf_op jit(solution)/shard_map/ppermute | solution.py:14
  10.3 1.9 multiply_reduce_fusion
  13.0 0.0 copy-start
  13.0 0.0 copy-done.1
  13.0 1.2 broadcast_divide_fusion
  14.3 72.5 %collective-permute-done = bf16[32,7,8192]{2,0,1:T(8,128)(2,1)} collective-permute-done((bf16[32,7,8192]{2,0,1:T(8,128)(2,1)}, bf16[32,7,8192]{2,0,1:T(8,128)(2,1)}, u32[]{:S(2)}, u32[]{:S(2)}) %collective-permute-start) | collective-permute-done | bytes 3670048 | tf_op jit(solution)/shard_map/ppermute | solution.py:14
  86.8 2.3 %constant_dynamic-update-slice_fusion.1 = bf16[32,15,8192]{2,0,1:T(8,128)(2,1)S(1)} fusion(bf16[32,7,8192]{2,0,1:T(8,128)(2,1)} %collective-permute-done), kind=kLoop, calls=%fused_computation.69 | loop fusion | bytes 7340032
  89.1 0.0 copy-done
  89.1 0.4 constant_dynamic-update-slice_fusion
  89.6 7.9 %multiply_add_fusion = f32[32,8,8192]{2,0,1:T(8,128)S(1)} fusion(bf16[32,15,8192]{2,0,1:T(8,128)(2,1)S(1)} %constant_dynamic-update-slice_fusion, f32[8192]{0:T(1024)S(1)} %get-tuple-element.10, f32[8192]{0:T(1024)S(1)} %get-tuple-element.11, f32[8192]{0:T(1024)S(1)} %get-tuple-element.12, f32[8192]{0:T(1024)S(1)} %get-tuple-element.13, ...), kind=kLoop, calls=%fused_computation.12 | loop fusion | flops 48234496 | bytes 42205184 | tf_op jit(solution)/shard_map/add | solution.py:46
  97.5 38.5 %fusion.5 = f32[256,32,8]{0,1,2:T(8,128)S(1)} fusion(f32[32,8,8192]{2,0,1:T(8,128)S(1)} %multiply_add_fusion, s32[256]{0:T(256)S(1)} %iota_add_fusion.2), kind=kOutput, calls=%fused_computation.9 | convolution fusion | flops 6471811072 | bytes 8651776 | tf_op jit(solution)/shard_map/ifm,mk->kif/dot_general | solution.py:38
  136.0 38.8 %subtract_convert_fusion = (bf16[256,32,8]{0,1,2:T(8,128)(2,1)S(1)}, bf16[256,32,8]{0,1,2:T(8,128)(2,1)S(1)}) fusion(f32[256,32,8]{0,1,2:T(8,128)S(1)} %fusion.5, f32[256,32]{0,1:T(8,128)S(1)} %get-tuple-element.18, f32[256,32]{0,1:T(8,128)S(1)} %get-tuple-element.17, f32[32,8,8192]{2,0,1:T(8,128)S(1)} %multiply_add_fusion, s32[256]{0:T(256)S(1)} %iota_add_fusion.2), kind=kOutput, calls=%fused_computation.63 | convolution fusion | flops 6472400896 | bytes 8979456 | tf_op jit(solution)/shard_map/ifm,mk->kif/dot_general | solution.py:39
  174.8 0.3 copy.25
  175.1 0.3 copy.26
  175.4 0.2 fusion.57
  175.6 1.0 reshape.144
  176.6 12.0 %all_to_all.27 = bf16[8,2,8192]{2,1,0:T(2,128)(2,1)S(1)} all-to-all(bf16[8,2,8192]{2,1,0:T(2,128)(2,1)S(1)} %reshape.144), channel_id=1, replica_groups=mesh['tm'=8,'stn'=32] {'tm'}, dimensions={0} | all-to-all | bytes 524288 | tf_op jit(solution)/shard_map/all_to_all | solution.py:88
  188.5 0.5 reshape.145
  189.0 0.3 copy_bitcast_fusion.1
  189.3 0.4 copy.24
  189.7 0.4 reshape.146
  190.1 26.8 %all_to_all.28 = bf16[32,2,2048]{2,1,0:T(2,128)(2,1)S(1)} all-to-all(bf16[32,2,2048]{2,1,0:T(2,128)(2,1)S(1)} %reshape.146), channel_id=1, replica_groups=mesh['tm'=8,'stn'=32] {'stn'}, dimensions={0} | all-to-all | bytes 524288 | tf_op jit(solution)/shard_map/all_to_all | solution.py:87
  216.9 0.4 reshape.147
  217.3 0.1 neg.22
  217.3 0.8 convolution_bitcast_fusion.1
  218.2 0.8 convolution_bitcast_fusion
  219.0 4.4 %maximum_multiply_fusion = f32[1,2,1024,1024]{3,2,1,0:T(8,128)} fusion(f32[1,1,1024,1024]{3,2,1,0:T(8,128)S(1)} %convolution_bitcast_fusion, f32[1,1,1024,1024]{3,2,1,0:T(8,128)S(1)} %convolution_bitcast_fusion.1), kind=kLoop, calls=%fused_computation.6 | loop fusion | flops 4194304 | bytes 16777216 | tf_op jit(solution)/shard_map/div | solution.py:61
  (4 shorter events, 0.1 us)
Async XLA Ops:
  0.0 13.0 %copy-start.1 = (f32[2,32,256]{2,1,0:T(8,128)S(1)}, f32[2,32,256]{2,1,0:T(8,128)}, u32[]{:S(2)}) copy-start(f32[2,32,256]{2,1,0:T(8,128)} %param.3) | copy-start | bytes 196612
  4.6 82.2 %collective-permute-start = (bf16[32,7,8192]{2,0,1:T(8,128)(2,1)}, bf16[32,7,8192]{2,0,1:T(8,128)(2,1)}, u32[]{:S(2)}, u32[]{:S(2)}) collective-permute-start(bf16[32,7,8192]{2,0,1:T(8,128)(2,1)} %slice.94), channel_id=1, source_target_pairs={{0,32},{32,64},{64,96},{96,128},{128,160},{160,192},{192,224},{1,3... | collective-permute-start | bytes 11010056 | tf_op jit(solution)/shard_map/ppermute | solution.py:14
  13.0 76.1 %copy-start = (bf16[32,65536]{1,0:T(8,128)(2,1)S(1)}, bf16[32,65536]{1,0:T(8,128)(2,1)}, u32[]{:S(2)}) copy-start(bf16[32,65536]{1,0:T(8,128)(2,1)} %param.2) | copy-start | bytes 12582916
where the time goes:
time: 224 us; the launch traced here: 223 us
  matrix products  78.9 us (35%)
  waiting for transfers between devices  72.5 us (32%)
  blocking collectives  38.7 us (17%)
  other arithmetic  15.7 us (7%)
  local copies, waits for them, and re-layouts  10.8 us (5%)
  starting transfers between devices  5.72 us (3%)
    ppermute x1, waiting for transfers between devices, passed_along(): return lax.ppermute(x, axis, pairs)  72.5 us
    dot_general x1, matrix products, band_spectra(): jnp.einsum('ifm,mk->kif', windowed, sin_table, precision=highest)  38.8 us
    dot_general x1, matrix products, band_spectra(): jnp.einsum('ifm,mk->kif', windowed, cos_table, precision=highest)  38.5 us
    all_to_all x1, blocking collectives, on_device(): lax.all_to_all(lax.all_to_all(blocks, 'tm', split_axis=1, concat_axis=5,...  26.8 us
    all_to_all x1, blocking collectives, on_device(): lax.all_to_all(blocks, 'tm', split_axis=1, concat_axis=5, tiled=True)  12 us
    add x1, other arithmetic, apply_taps(): windowed + window[tap_index] * extended[:, tap_index:tap_index + frames,...  7.9 us
    ppermute x1, starting transfers between devices, passed_along(): return lax.ppermute(x, axis, pairs)  5.72 us
  transfers between devices with their start and end apart: 1, of which 1 were waited for; matrix products, arithmetic and copies ran while one was open for 1% of the time, Pallas kernels for 0%

commit v1 on v0

v1 whole, which is shorter than its diff:
```python
import numpy as np

import jax
import jax.numpy as jnp
from jax import lax
from jax.sharding import PartitionSpec as P

CHANNELS = 4096
BAND_LOW = 1024
TAPS = 8


def passed_along(x, axis, by):
    devices = lax.axis_size(axis)
    pairs = [(i, i + by) for i in range(devices) if 0 <= i + by < devices]
    return lax.ppermute(x, axis, pairs)


def window_table(chans):
    frame_len = 2 * chans
    total_len = TAPS * frame_len
    positions = np.arange(total_len, dtype=np.float64)
    centred = (positions - (total_len - 1) / 2.0) / frame_len
    taper = np.sin(np.pi * (positions + 0.5) / total_len)
    shaped = np.sinc(centred) * taper * taper
    shaped = shaped / np.sqrt(np.sum(shaped * shaped))
    return shaped.reshape(TAPS, frame_len).astype(np.float32)


def split(x):
    hi = lax.reduce_precision(x, exponent_bits=8, mantissa_bits=7)
    lo = x - hi
    return hi.astype(jnp.bfloat16), lo.astype(jnp.bfloat16)


def band_tables(frame_len, band):
    half = band // 2
    n_b = 32
    n_a = frame_len // 2 // n_b
    q = jnp.arange(2, dtype=jnp.int32)[:, None, None]
    k = jnp.arange(band, dtype=jnp.int32)[None, None, :]
    chan = 2 * (k % half) + q
    imag_col = k >= half
    a = jnp.arange(n_a, dtype=jnp.int32)[None, :, None]
    b = jnp.arange(n_b, dtype=jnp.int32)[None, :, None]
    p_steps = n_a * 2
    tp = (2.0 * jnp.pi / p_steps) * ((a * chan) % p_steps).astype(jnp.float32)
    tq = (2.0 * jnp.pi / frame_len) * ((b * (BAND_LOW + chan)) % frame_len).astype(jnp.float32)
    pr, pi = jnp.cos(tp), -jnp.sin(tp)
    qr, qi = jnp.cos(tq), -jnp.sin(tq)
    b1 = jnp.where(imag_col, qi, qr)
    b2 = jnp.where(imag_col, qr, -qi)
    t = pr[:, :, None, :] * b1[:, None, :, :] + pi[:, :, None, :] * b2[:, None, :, :]
    return split(t.reshape(2, n_a * n_b, band))


def on_device(voltages, gains):
    in_dev, length = voltages.shape
    band = gains.shape[2]
    half_band = band // 2
    frame_len = 2 * CHANNELS
    half_len = frame_len // 2
    frames = length // frame_len
    n_time = lax.axis_size("tm")
    n_station = lax.axis_size("stn")
    all_inputs = in_dev * n_station
    history = TAPS - 1
    slots = frames + history
    window = jnp.asarray(window_table(CHANNELS))
    t_hi, t_lo = band_tables(frame_len, band)

    framed = voltages.reshape(in_dev, frames, frame_len)
    pad = jnp.zeros((in_dev, history, frame_len), voltages.dtype)
    padded = jnp.concatenate([pad, framed, pad], axis=1).astype(jnp.float32)
    windowed = window[0] * padded[:, 0:slots, :]
    for tap_index in range(1, TAPS):
        windowed = windowed + window[tap_index] * padded[:, tap_index : tap_index + slots, :]
    first, second = windowed[..., :half_len], windowed[..., half_len:]
    folded = jnp.stack([first + second, first - second])
    l_hi, l_lo = split(folded)
    lhs = jnp.stack([l_hi, l_lo], axis=1)
    f32 = jnp.float32
    part_hi = jnp.einsum("qhism,qmk->qhisk", lhs, t_hi, preferred_element_type=f32)
    part_lo = jnp.einsum("qism,qmk->qisk", l_hi, t_lo, preferred_element_type=f32)
    raw = (part_hi[:, 0] + part_hi[:, 1]) + part_lo

    own = raw[:, :, :frames, :]
    given = passed_along(raw[:, :, frames:, :], "tm", 1)
    own = own.at[:, :, :history, :].add(given)

    own = own.reshape(2, in_dev, frames, 2, half_band)
    raw_re = jnp.transpose(own[:, :, :, 0, :], (3, 0, 1, 2))
    raw_im = jnp.transpose(own[:, :, :, 1, :], (3, 0, 1, 2))
    g = jnp.transpose(gains.reshape(2, in_dev, half_band, 2), (0, 2, 3, 1))[..., None]
    gain_re, gain_im = g[0], g[1]
    spec_re = gain_re * raw_re - gain_im * raw_im
    spec_im = gain_re * raw_im + gain_im * raw_re
    spectra = jnp.stack([spec_re, spec_im], axis=3).astype(jnp.bfloat16)
    row = in_dev * 2 * frames
    spectra = spectra.reshape(n_time, n_station, row)
    spectra = lax.all_to_all(spectra, "tm", split_axis=0, concat_axis=0, tiled=True)
    spectra = lax.all_to_all(spectra, "stn", split_axis=1, concat_axis=1, tiled=True)
    spectra = spectra.reshape(n_time, n_station, in_dev, 2, frames)
    spectra = jnp.transpose(spectra, (1, 2, 3, 0, 4)).reshape(all_inputs, 2, n_time * frames)
    stacked = spectra.reshape(all_inputs, 2 * n_time * frames)
    flipped = jnp.concatenate([spectra[:, 1], -spectra[:, 0]], axis=-1)
    both = jnp.concatenate([stacked, flipped], axis=0)
    vis = jnp.einsum("ik,jk->ij", both, stacked, preferred_element_type=f32)
    vis = vis * (1.0 / float(n_time * frames))
    return vis.reshape(1, 2, all_inputs, all_inputs)


def solution(mesh):
    in_specs = (P("stn", "tm"), P(None, "stn", None))
    out_specs = P(("tm", "stn"), None, None, None)
    return jax.shard_map(
        on_device, mesh=mesh, in_specs=in_specs, out_specs=out_specs, check_vma=False
    )
```

time: 224 us -> 175 us (0.78)
  other arithmetic: 15.7 us -> 84.9 us
  waiting for transfers between devices: 72.5 us -> 8.58 us
  matrix products: 78.9 us -> 19.1 us
  local copies, waits for them, and re-layouts: 10.8 us -> 19.4 us
    ppermute x1, waiting for transfers between devices: 72.5 us -> 8.58 us  [passed_along(): return lax.ppermute(x, axis, pairs)]
    dot_general x4 -> x3, matrix products: 78.9 us -> 19.1 us  [the longest x1 7.27 us: on_device(): jnp.einsum('qism,qmk->qisk', l_hi, t_lo, preferred_element_type=f32)]
    add x2 -> x3, other arithmetic: 7.91 us -> 51.3 us  [the longest x1 50 us: on_device(): windowed + window[tap_index] * padded[:, tap_index:tap_index + slots, :]]
    convert_element_type x0 -> x3, other arithmetic: none -> 18.7 us  [the longest x2 10.7 us: split(): return (hi.astype(jnp.bfloat16), lo.astype(jnp.bfloat16))]
    another operation x0 -> x3, other arithmetic: none -> 13.6 us  [the longest x1 13.2 us: on_device(): folded = jnp.stack([first + second, first - second])]
    another operation x2, local copies, waits for them, and re-layouts: 0.62 us -> 7.81 us  [the longest x1 6.72 us: on_device(): spectra = jnp.stack([spec_re, spec_im], axis=3).astype(jnp.bfloat16)]
    convert_element_type x0 -> x1, local copies, waits for them, and re-layouts: none -> 7.05 us  [on_device(): spectra = jnp.stack([spec_re, spec_im], axis=3).astype(jnp.bfloat16)]
    div x2 -> x0, other arithmetic: 5.63 us -> none  [the longest x1 4.39 us: cross_power(): return jnp.stack([vis_real, vis_imag], axis=1) / total_frames]
  transfers between devices with their start and end apart: 1 -> 1, of which waited for: 1 -> 1; matrix products, arithmetic and copies ran while one was open for 1% -> 0% of each run, Pallas kernels for 0% -> 0%
where the time goes in v1:
time: 175 us
  other arithmetic  84.9 us (49%)
  blocking collectives  38.7 us (22%)
  local copies, waits for them, and re-layouts  19.4 us (11%)
  matrix products  19.1 us (11%)
  waiting for transfers between devices  8.58 us (5%)
  starting transfers between devices  4.18 us (2%)
    add x1, other arithmetic, on_device(): windowed + window[tap_index] * padded[:, tap_index:tap_index + slots, :]  50 us
    all_to_all x1, blocking collectives, on_device(): lax.all_to_all(spectra, 'stn', split_axis=1, concat_axis=1, tiled=True)  26.8 us
    another operation x1, other arithmetic, on_device(): folded = jnp.stack([first + second, first - second])  13.2 us
    all_to_all x1, blocking collectives, on_device(): lax.all_to_all(spectra, 'tm', split_axis=0, concat_axis=0, tiled=True)  11.9 us
    convert_element_type x2, other arithmetic, split(): return (hi.astype(jnp.bfloat16), lo.astype(jnp.bfloat16))  10.7 us
    ppermute x1, waiting for transfers between devices, passed_along(): return lax.ppermute(x, axis, pairs)  8.58 us
    convert_element_type x1, other arithmetic, on_device(): padded = jnp.concatenate([pad, framed, pad], axis=1).astype(jnp.float32)  7.96 us
    dot_general x1, matrix products, on_device(): jnp.einsum('qism,qmk->qisk', l_hi, t_lo, preferred_element_type=f32)  7.27 us
  transfers between devices with their start and end apart: 1, of which 1 were waited for; matrix products, arithmetic and copies ran while one was open for 0% of the time, Pallas kernels for 0%

profile of v1, /device:TPU:1, one launch (start us, length us, event | category | flops | bytes accessed | tf_op | source)
XLA Modules:
  0.0 175.2 jit_solution(2518422193169905856)
XLA Ops:
  0.0 1.0 fusion.43
  1.1 0.3 negate_select_fusion.4
  1.4 1.2 multiply_add_fusion
  2.6 0.0 copy-start.1
  2.6 5.4 %reduce-precision_convert_fusion.1 = (bf16[2,4096,256]{2,1,0:T(8,128)(2,1)}, bf16[2,4096,256]{2,1,0:T(8,128)(2,1)}) fusion(f32[2,128,32,256]{3,2,1,0:T(8,128)S(1)} %multiply_add_fusion), kind=kLoop, calls=%fused_computation.26 | loop fusion | flops 8388608 | bytes 16777216 | tf_op jit(solution)/shard_map/convert_element_type | solution.py:33
  8.0 0.0 copy-done.1
  8.0 0.3 copy.60
  8.3 0.4 broadcast_in_dim.15
  8.7 0.0 copy-start.3
  8.7 0.0 copy-start.4
  8.7 0.0 copy-start.5
  8.7 0.0 copy-start.6
  8.7 0.0 copy-start.7
  8.7 0.0 copy-start.8
  8.7 0.0 copy-start.9
  8.8 0.0 copy-start.10
  8.8 8.0 %maximum_convert_fusion = f32[32,22,8192]{2,0,1:T(8,128)} fusion(bf16[32,7,8192]{2,0,1:T(8,128)(2,1)S(1)} %broadcast_in_dim.15, bf16[32,8,8192]{2,0,1:T(8,128)(2,1)S(1)} %bitcast.87), kind=kLoop, calls=%fused_computation.27 | loop fusion | flops 17301504 | bytes 30932992 | tf_op jit(solution)/shard_map/convert_element_type | solution.py:74
  16.7 0.0 copy-done.3
  16.7 0.0 copy-done.4
  16.7 0.0 copy-done.5
  16.7 0.0 copy-done.6
  16.8 0.0 copy-done.7
  16.8 0.0 copy-done.8
  16.8 0.0 copy-done.9
  16.8 0.0 copy-done.10
  16.8 50.0 %fusion.1 = f32[32,15,8192]{2,0,1:T(8,128)} fusion(f32[32,22,8192]{2,0,1:T(8,128)} %maximum_convert_fusion, f32[8192]{0:T(1024)S(1)} %copy-done.3, f32[8192]{0:T(1024)S(1)} %copy-done.4, f32[8192]{0:T(1024)S(1)} %copy-done.5, f32[8192]{0:T(1024)S(1)} %copy-done.6, f32[8192]{0:T(1024)S(1)} %copy-done.7, f32[8192]{0:T(1024)S(1)} %copy-done.8, ...), kind=kLoop, calls=%fused_computation.4 | loop fusion | flops 58982400 | bytes 141819904 | tf_op jit(solution)/shard_map/add | solution.py:77
  66.8 13.2 %fusion.19 = (f32[1,1,32,15,4096]{4,2,3,1,0:T(8,128)S(1)}, f32[1,32,15,4096]{3,1,2,0:T(8,128)}, f32[1,32,15,4096]{3,1,2,0:T(8,128)}, f32[1,1,32,15,4096]{4,2,3,1,0:T(8,128)}) fusion(f32[32,15,8192]{2,0,1:T(8,128)} %fusion.1), kind=kLoop, calls=%fused_computation.38 | loop fusion | flops 3932160 | bytes 47185920 | tf_op jit(solution)/shard_map/stack | solution.py:79
  80.0 5.3 %reduce-precision_convert_fusion = (bf16[2,1,32,15,4096]{4,2,3,1,0:T(8,128)(2,1)S(1)}, bf16[2,1,32,15,4096]{4,2,3,1,0:T(8,128)(2,1)S(1)}) fusion(f32[1,1,32,15,4096]{4,2,3,1,0:T(8,128)} %get-tuple-element.22, f32[1,1,32,15,4096]{4,2,3,1,0:T(8,128)S(1)} %get-tuple-element.19), kind=kLoop, calls=%fused_computation.1 | loop fusion | flops 19660800 | bytes 31457280 | tf_op jit(solution)/shard_map/convert_element_type | solution.py:33
  85.4 0.0 copy-start
  85.4 7.1 %fusion.8 = f32[2,2,32,15,256]{4,2,3,1,0:T(8,128)} fusion(bf16[2,1,32,15,4096]{4,2,3,1,0:T(8,128)(2,1)S(1)} %get-tuple-element.18, bf16[2,1,32,15,4096]{4,2,3,1,0:T(8,128)(2,1)S(1)} %get-tuple-element.17, bf16[2,4096,256]{2,1,0:T(8,128)(2,1)} %get-tuple-element.23), kind=kOutput, calls=%fused_computation.19 | convolution fusion | flops 4034396160 | bytes 21889024 | tf_op jit(solution)/shard_map/qhism,qmk->qhisk/dot_general | solution.py:83
  92.5 0.0 copy-done
  92.5 0.0 copy-start.2
  92.5 7.3 %fusion.22 = f32[2,32,15,256]{3,1,2,0:T(8,128)S(1)} fusion(bf16[2,4096,256]{2,1,0:T(8,128)(2,1)} %get-tuple-element.24, f32[1,32,15,4096]{3,1,2,0:T(8,128)S(1)} %copy-done, f32[1,32,15,4096]{3,1,2,0:T(8,128)} %get-tuple-element.21, f32[2,2,32,15,256]{4,2,3,1,0:T(8,128)} %fusion.8), kind=kOutput, calls=%fused_computation.41 | convolution fusion | flops 2025553920 | bytes 22872064 | tf_op jit(solution)/shard_map/qism,qmk->qisk/dot_general | solution.py:84
  99.8 4.2 %collective-permute-start = (f32[2,32,7,256]{3,1,2,0:T(8,128)S(1)}, f32[2,32,7,256]{3,1,2,0:T(8,128)S(1)}, u32[]{:S(2)}, u32[]{:S(2)}) collective-permute-start(f32[2,32,7,256]{3,1,2,0:T(8,128)S(1)} %slice.160), channel_id=1, source_target_pairs={{0,32},{32,64},{64,96},{96,128},{128,160},{160,192},{192,224},{1,3... | collective-permute-start | bytes 1376264 | tf_op jit(solution)/shard_map/ppermute | solution.py:16
  104.0 0.0 copy-done.2
  104.1 0.1 copy.25
  104.2 0.1 copy.29
  104.3 0.1 copy.26
  104.4 8.6 %collective-permute-done = f32[2,32,7,256]{3,1,2,0:T(8,128)S(1)} collective-permute-done((f32[2,32,7,256]{3,1,2,0:T(8,128)S(1)}, f32[2,32,7,256]{3,1,2,0:T(8,128)S(1)}, u32[]{:S(2)}, u32[]{:S(2)}) %collective-permute-start) | collective-permute-done | bytes 458784 | tf_op jit(solution)/shard_map/ppermute | solution.py:16
  112.9 0.1 fusion.33
  113.0 0.3 reshape.268
  113.3 0.6 fusion.57
  113.8 0.3 fusion.40
  114.2 6.7 %copy.31 = bf16[128,2,32,2,8]{4,3,2,1,0:T(2,128)(2,1)} copy(bf16[128,2,32,2,8]{0,4,3,2,1:T(8,128)(2,1)S(1)} %pad_maximum_fusion.1) | data formatting | bytes 524288 | tf_op jit(solution)/shard_map/stack | solution.py:98
  121.0 7.0 %convert_element_type.68 = bf16[8,32,512]{2,1,0:T(8,128)(2,1)S(1)} reshape(bf16[128,2,32,2,8]{4,3,2,1,0:T(2,128)(2,1)} %copy.31) | data formatting | bytes 524288 | tf_op jit(solution)/shard_map/convert_element_type | solution.py:98
  128.0 11.9 %all_to_all.10 = bf16[8,32,512]{2,1,0:T(8,128)(2,1)S(1)} all-to-all(bf16[8,32,512]{2,1,0:T(8,128)(2,1)S(1)} %convert_element_type.68), channel_id=1, replica_groups=mesh['tm'=8,'stn'=32] {'tm'}, dimensions={0} | all-to-all | bytes 524288 | tf_op jit(solution)/shard_map/all_to_all | solution.py:101
  140.0 0.1 copy.32
  140.1 26.8 %all_to_all.11 = bf16[8,32,512]{2,0,1:T(8,128)(2,1)S(1)} all-to-all(bf16[8,32,512]{2,0,1:T(8,128)(2,1)S(1)} %copy.32), channel_id=1, replica_groups=mesh['tm'=8,'stn'=32] {'stn'}, dimensions={1} | all-to-all | bytes 524288 | tf_op jit(solution)/shard_map/all_to_all | solution.py:102
  166.9 0.5 copy.33
  167.4 0.9 copy.34
  168.3 1.1 reshape_reshape.3
  169.4 1.1 reshape.270
  170.5 4.7 %convolution_multiply_fusion = f32[2048,1024]{1,0:T(8,128)} fusion(bf16[1024,128]{0,1:T(8,128)(2,1)S(1)} %reshape_reshape.3, bf16[1024,64]{0,1:T(8,128)(2,1)S(1)} %get-tuple-element.30, bf16[1024,64]{0,1:T(8,128)(2,1)S(1)} %get-tuple-element.29), kind=kOutput, calls=%fused_computation.33 | convolution fusion | flops 540540928 | bytes 8912896 | tf_op jit(solution)/shard_map/ik,jk->ij/dot_general | solution.py:108
  (8 shorter events, 0.2 us)
Async XLA Ops:
  2.6 5.4 %copy-start.1 = (bf16[32,65536]{1,0:T(8,128)(2,1)S(1)}, bf16[32,65536]{1,0:T(8,128)(2,1)}, u32[]{:S(2)}) copy-start(bf16[32,65536]{1,0:T(8,128)(2,1)} %param.5) | copy-start | bytes 12582916
  8.7 8.1 %copy-start.3 = (f32[8192]{0:T(1024)S(1)}, f32[8192]{0:T(1024)}, u32[]{:S(2)}) copy-start(f32[8192]{0:T(1024)} %constant.101) | copy-start | bytes 98308
  8.7 8.1 %copy-start.4 = (f32[8192]{0:T(1024)S(1)}, f32[8192]{0:T(1024)}, u32[]{:S(2)}) copy-start(f32[8192]{0:T(1024)} %constant.99) | copy-start | bytes 98308
  8.7 8.0 %copy-start.5 = (f32[8192]{0:T(1024)S(1)}, f32[8192]{0:T(1024)}, u32[]{:S(2)}) copy-start(f32[8192]{0:T(1024)} %constant.97) | copy-start | bytes 98308
  8.7 8.0 %copy-start.6 = (f32[8192]{0:T(1024)S(1)}, f32[8192]{0:T(1024)}, u32[]{:S(2)}) copy-start(f32[8192]{0:T(1024)} %constant.95) | copy-start | bytes 98308
  8.7 8.0 %copy-start.7 = (f32[8192]{0:T(1024)S(1)}, f32[8192]{0:T(1024)}, u32[]{:S(2)}) copy-start(f32[8192]{0:T(1024)} %constant.93) | copy-start | bytes 98308
  8.7 8.0 %copy-start.8 = (f32[8192]{0:T(1024)S(1)}, f32[8192]{0:T(1024)}, u32[]{:S(2)}) copy-start(f32[8192]{0:T(1024)} %constant.91) | copy-start | bytes 98308
  8.7 8.0 %copy-start.9 = (f32[8192]{0:T(1024)S(1)}, f32[8192]{0:T(1024)}, u32[]{:S(2)}) copy-start(f32[8192]{0:T(1024)} %constant.89) | copy-start | bytes 98308
  8.8 8.0 %copy-start.10 = (f32[8192]{0:T(1024)S(1)}, f32[8192]{0:T(1024)}, u32[]{:S(2)}) copy-start(f32[8192]{0:T(1024)} %constant.87) | copy-start | bytes 98308
  85.4 7.1 %copy-start = (f32[1,32,15,4096]{3,1,2,0:T(8,128)S(1)}, f32[1,32,15,4096]{3,1,2,0:T(8,128)}, u32[]{:S(2)}) copy-start(f32[1,32,15,4096]{3,1,2,0:T(8,128)} %get-tuple-element.20) | copy-start | bytes 23592964
  92.5 11.6 %copy-start.2 = (f32[2,32,256]{2,1,0:T(8,128)S(1)}, f32[2,32,256]{2,1,0:T(8,128)}, u32[]{:S(2)}) copy-start(f32[2,32,256]{2,1,0:T(8,128)} %param.6) | copy-start | bytes 196612
  99.8 13.1 %collective-permute-start = (f32[2,32,7,256]{3,1,2,0:T(8,128)S(1)}, f32[2,32,7,256]{3,1,2,0:T(8,128)S(1)}, u32[]{:S(2)}, u32[]{:S(2)}) collective-permute-start(f32[2,32,7,256]{3,1,2,0:T(8,128)S(1)} %slice.160), channel_id=1, source_target_pairs={{0,32},{32,64},{64,96},{96,128},{128,160},{160,192},{192,224},{1,3... | collective-permute-start | bytes 1376264 | tf_op jit(solution)/shard_map/ppermute | solution.py:16

commit v2 on v1

v2 whole, which is shorter than its diff:
```python
import numpy as np

import jax
import jax.numpy as jnp
from jax import lax
from jax.experimental import pallas as pl
from jax.experimental.pallas import tpu as pltpu
from jax.sharding import PartitionSpec as P

CHANNELS = 4096
BAND_LOW = 1024
TAPS = 8


def passed_along(x, axis, by):
    devices = lax.axis_size(axis)
    pairs = [(i, i + by) for i in range(devices) if 0 <= i + by < devices]
    return lax.ppermute(x, axis, pairs)


def window_table(chans):
    frame_len = 2 * chans
    total_len = TAPS * frame_len
    positions = np.arange(total_len, dtype=np.float64)
    centred = (positions - (total_len - 1) / 2.0) / frame_len
    taper = np.sin(np.pi * (positions + 0.5) / total_len)
    shaped = np.sinc(centred) * taper * taper
    shaped = shaped / np.sqrt(np.sum(shaped * shaped))
    return shaped.reshape(TAPS, frame_len).astype(np.float32)


def split(x):
    hi = lax.reduce_precision(x, exponent_bits=8, mantissa_bits=7)
    lo = x - hi
    return hi.astype(jnp.bfloat16), lo.astype(jnp.bfloat16)


def band_tables(frame_len, band):
    half = band // 2
    n_b = 32
    n_a = frame_len // 2 // n_b
    q = jnp.arange(2, dtype=jnp.int32)[:, None, None]
    k = jnp.arange(band, dtype=jnp.int32)[None, None, :]
    chan = 2 * (k % half) + q
    imag_col = k >= half
    a = jnp.arange(n_a, dtype=jnp.int32)[None, :, None]
    b = jnp.arange(n_b, dtype=jnp.int32)[None, :, None]
    p_steps = n_a * 2
    tp = (2.0 * jnp.pi / p_steps) * ((a * chan) % p_steps).astype(jnp.float32)
    tq = (2.0 * jnp.pi / frame_len) * ((b * (BAND_LOW + chan)) % frame_len).astype(jnp.float32)
    pr, pi = jnp.cos(tp), -jnp.sin(tp)
    qr, qi = jnp.cos(tq), -jnp.sin(tq)
    b1 = jnp.where(imag_col, qi, qr)
    b2 = jnp.where(imag_col, qr, -qi)
    t = pr[:, :, None, :] * b1[:, None, :, :] + pi[:, :, None, :] * b2[:, None, :, :]
    return split(t.reshape(2, n_a * n_b, band))


def taps_kernel(x_ref, w_ref, own_ref, next_ref):
    frame_len = w_ref.shape[1]
    half = frame_len // 2
    frames = x_ref.shape[1] // frame_len
    history = TAPS - 1
    lanes = 128

    def chunk(j, carry):
        base = pl.multiple_of(j * lanes, lanes)
        xs = []
        ws = []
        for offset in (0, half):
            xs.append([x_ref[:, pl.ds(f * frame_len + offset + base, lanes)].astype(jnp.float32) for f in range(frames)])
            ws.append([w_ref[pl.ds(p, 1), pl.ds(offset + base, lanes)] for p in range(TAPS)])
        for s in range(frames + history):
            accs = []
            for part in range(2):
                acc = None
                for p in range(TAPS):
                    g = s + p - history
                    if 0 <= g < frames:
                        term = ws[part][p] * xs[part][g]
                        acc = term if acc is None else acc + term
                accs.append(acc)
            folded = (accs[0] + accs[1], accs[0] - accs[1])
            ref, slot = (own_ref, s) if s < frames else (next_ref, s - frames)
            for q in range(2):
                hi = folded[q].astype(jnp.bfloat16)
                lo = (folded[q] - hi.astype(jnp.float32)).astype(jnp.bfloat16)
                ref[q, 0, slot, :, pl.ds(base, lanes)] = hi
                ref[q, 1, slot, :, pl.ds(base, lanes)] = lo
        return carry

    lax.fori_loop(0, half // lanes, chunk, 0)


def windowed_parts(voltages, window, frames):
    in_dev, length = voltages.shape
    frame_len = window.shape[1]
    half = frame_len // 2
    history = TAPS - 1
    block = 16
    out_shape = (
        jax.ShapeDtypeStruct((2, 2, frames, in_dev, half), jnp.bfloat16),
        jax.ShapeDtypeStruct((2, 2, history, in_dev, half), jnp.bfloat16),
    )
    return pl.pallas_call(
        taps_kernel,
        out_shape=out_shape,
        grid=(in_dev // block,),
        in_specs=[
            pl.BlockSpec((block, length), lambda g: (g, 0)),
            pl.BlockSpec((TAPS, frame_len), lambda g: (0, 0)),
        ],
        out_specs=[
            pl.BlockSpec((2, 2, frames, block, half), lambda g: (0, 0, 0, g, 0)),
            pl.BlockSpec((2, 2, history, block, half), lambda g: (0, 0, 0, g, 0)),
        ],
        compiler_params=pltpu.CompilerParams(vmem_limit_bytes=48 * 1024 * 1024),
    )(voltages, window)


def band_dft(parts, t_hi, t_lo):
    q, h, slots, inputs, m = parts.shape
    lhs = parts.reshape(q, h, slots * inputs, m)
    f32 = jnp.float32
    both = jnp.einsum("qhrm,qmk->qhkr", lhs, t_hi, preferred_element_type=f32)
    high = jnp.einsum("qrm,qmk->qkr", lhs[:, 0], t_lo, preferred_element_type=f32)
    return (both[:, 0] + both[:, 1]) + high


def on_device(voltages, gains):
    in_dev, length = voltages.shape
    band = gains.shape[2]
    half_band = band // 2
    frame_len = 2 * CHANNELS
    frames = length // frame_len
    n_time = lax.axis_size("tm")
    n_station = lax.axis_size("stn")
    all_inputs = in_dev * n_station
    history = TAPS - 1
    window = jnp.asarray(window_table(CHANNELS))
    t_hi, t_lo = band_tables(frame_len, band)

    own_parts, next_parts = windowed_parts(voltages, window, frames)
    raw_next = band_dft(next_parts, t_hi, t_lo)
    given = passed_along(raw_next, "tm", 1)
    raw = band_dft(own_parts, t_hi, t_lo)
    raw = raw.at[:, :, : history * in_dev].add(given)

    row = frames * in_dev
    raw = jnp.transpose(raw.reshape(2, 2, half_band, row), (1, 2, 0, 3))
    raw_re, raw_im = raw[0], raw[1]
    g = jnp.transpose(gains.reshape(2, in_dev, half_band, 2), (0, 2, 3, 1))
    g = jnp.tile(g, (1, 1, 1, frames))
    gain_re, gain_im = g[0], g[1]
    spec_re = gain_re * raw_re - gain_im * raw_im
    spec_im = gain_re * raw_im + gain_im * raw_re
    spectra = jnp.stack([spec_re, spec_im], axis=2).astype(jnp.bfloat16)
    spectra = spectra.reshape(n_time * n_station, 2 * row)
    spectra = lax.all_to_all(spectra, ("tm", "stn"), split_axis=0, concat_axis=0, tiled=True)
    spectra = spectra.reshape(n_time, n_station, 2, frames, in_dev)
    stacked = jnp.transpose(spectra, (2, 0, 3, 1, 4)).reshape(2, n_time * frames, all_inputs)
    flipped = jnp.concatenate([stacked[1], -stacked[0]], axis=0)
    stacked = stacked.reshape(2 * n_time * frames, all_inputs)
    both = jnp.concatenate([stacked, flipped], axis=1)
    vis = jnp.einsum("ki,kj->ij", both, stacked, preferred_element_type=jnp.float32)
    vis = vis * (1.0 / float(n_time * frames))
    return vis.reshape(1, 2, all_inputs, all_inputs)


def solution(mesh):
    in_specs = (P("stn", "tm"), P(None, "stn", None))
    out_specs = P(("tm", "stn"), None, None, None)
    return jax.shard_map(
        on_device, mesh=mesh, in_specs=in_specs, out_specs=out_specs, check_vma=False
    )
```

time: 175 us -> 92.5 us (0.53)
  other arithmetic: 84.9 us -> 11.8 us
  local copies, waits for them, and re-layouts: 19.4 us -> 7.08 us
  Pallas kernels: 0 us -> 10.9 us
  waiting for transfers between devices: 8.58 us -> 0.01 us
  matrix products: 19.1 us -> 27.5 us
  blocking collectives: 38.7 us -> 30.6 us
    add x1, other arithmetic: 50 us -> 0.07 us  [on_device(): raw = raw.at[:, :, :history * in_dev].add(given)]
    another operation x3 -> x2, other arithmetic: 13.6 us -> 0.1 us  [the longest x1 13.2 us: on_device(): folded = jnp.stack([first + second, first - second])]
    pallas_call x0 -> x1, Pallas kernels: none -> 10.9 us  [windowed_parts(): pl.pallas_call(taps_kernel, out_shape=out_shape, grid=(in_dev // block,),...]
    ppermute x1, waiting for transfers between devices: 8.58 us -> 0.01 us  [passed_along(): return lax.ppermute(x, axis, pairs)]
    dot_general x3 -> x5, matrix products: 19.1 us -> 27.5 us  [the longest x2 13.7 us: band_dft(): both = jnp.einsum('qhrm,qmk->qhkr', lhs, t_hi, preferred_element_type=f32)]
    all_to_all x2 -> x1, blocking collectives: 38.7 us -> 30.6 us  [on_device(): lax.all_to_all(spectra, ('tm', 'stn'), split_axis=0, concat_axis=0, tiled...]
    another operation x2, local copies, waits for them, and re-layouts: 7.81 us -> 1.28 us  [the longest x1 1.09 us: on_device(): stacked = stacked.reshape(2 * n_time * frames, all_inputs)]
    convert_element_type x1 -> x2, local copies, waits for them, and re-layouts: 7.05 us -> 0.75 us  [on_device(): spectra = jnp.stack([spec_re, spec_im], axis=2).astype(jnp.bfloat16)]
  transfers between devices with their start and end apart: 1 -> 1, of which waited for: 1 -> 0; matrix products, arithmetic and copies ran while one was open for 0% -> 13% of each run, Pallas kernels for 0% -> 0%
where the time goes in v2:
time: 92.5 us; the launch traced here: 92.4 us
  blocking collectives  30.6 us (33%)
  matrix products  27.5 us (30%)
  other arithmetic  11.8 us (13%)
  Pallas kernels  10.9 us (12%)
  local copies, waits for them, and re-layouts  7.08 us (8%)
  starting transfers between devices  4.15 us (4%)
    all_to_all x1, blocking collectives, on_device(): lax.all_to_all(spectra, ('tm', 'stn'), split_axis=0, concat_axis=0, tiled...  30.6 us
    dot_general x2, matrix products, band_dft(): both = jnp.einsum('qhrm,qmk->qhkr', lhs, t_hi, preferred_element_type=f32)  13.7 us
    pallas_call x1, Pallas kernels, windowed_parts(): pl.pallas_call(taps_kernel, out_shape=out_shape, grid=(in_dev // block,),...  10.9 us
    dot_general x2, matrix products, band_dft(): jnp.einsum('qrm,qmk->qkr', lhs[:, 0], t_lo, preferred_element_type=f32)  9.15 us
    convert_element_type x1, other arithmetic, split(): return (hi.astype(jnp.bfloat16), lo.astype(jnp.bfloat16))  5.16 us
    dot_general x1, matrix products, on_device(): jnp.einsum('ki,kj->ij', both, stacked, preferred_element_type=jnp.float32)  4.68 us
    ppermute x1, starting transfers between devices, passed_along(): return lax.ppermute(x, axis, pairs)  4.15 us
    convert_element_type x1, other arithmetic, on_device(): spectra = jnp.stack([spec_re, spec_im], axis=2).astype(jnp.bfloat16)  2.21 us
  transfers between devices with their start and end apart: 1, of which 0 were waited for; matrix products, arithmetic and copies ran while one was open for 13% of the time, Pallas kernels for 0%

profile of v2, /device:TPU:1, one launch (start us, length us, event | category | flops | bytes accessed | tf_op | source)
XLA Modules:
  0.0 92.4 jit_solution(9631384981227736693)
XLA Ops:
  0.0 1.0 %fusion.32 = (f32[2,128,256]{2,1,0:T(8,128)S(1)}, f32[2,128,256]{2,1,0:T(8,128)S(1)}) fusion(s32[2,256]{1,0:T(2,128)S(1)} %get-tuple-element.33), kind=kLoop, calls=%fused_computation.51 | loop fusion | flops 983040 | bytes 526336 | tf_op jit(solution)/shard_map/cos | solution.py:51
  1.1 0.3 negate_select_fusion.4
  1.4 1.2 %multiply_add_fusion = f32[2,128,32,256]{3,2,1,0:T(8,128)S(1)} fusion(f32[2,32,256]{2,1,0:T(8,128)S(1)} %get-tuple-element.30, f32[2,128,256]{2,1,0:T(8,128)S(1)} %get-tuple-element.32, f32[2,32,256]{2,1,0:T(8,128)S(1)} %get-tuple-element.29, f32[2,128,256]{2,1,0:T(8,128)S(1)} %get-tuple-element.31), kind=kLoop, calls=%fused_computation.3 | loop fusion | flops 6291456 | bytes 9043968 | tf_op jit(solution)/shard_map/add | solution.py:55
  2.6 0.0 copy-start
  2.6 0.0 copy-start.1
  2.6 5.2 %reduce-precision_convert_fusion = (bf16[2,4096,256]{2,1,0:T(8,128)(2,1)}, bf16[2,4096,256]{2,1,0:T(8,128)(2,1)}) fusion(f32[2,128,32,256]{3,2,1,0:T(8,128)S(1)} %multiply_add_fusion), kind=kLoop, calls=%fused_computation.1 | loop fusion | flops 8388608 | bytes 16777216 | tf_op jit(solution)/shard_map/convert_element_type | solution.py:35
  7.8 0.0 copy-done
  7.8 0.0 copy-done.1
  7.8 10.9 %shard_map.37 = (bf16[2,2,8,32,4096]{4,3,2,1,0:T(8,128)(2,1)}, bf16[2,2,7,32,4096]{4,3,2,1,0:T(8,128)(2,1)}) custom-call(bf16[32,65536]{1,0:T(8,128)(2,1)S(1)} %copy-done, f32[8,8192]{1,0:T(8,128)S(1)} %copy-done.1), custom_call_target="tpu_custom_call" | custom-call | tf_op jit(solution)/shard_map/pallas_call | solution.py:105
  18.7 0.0 copy-start.2
  18.7 7.4 %fusion.7 = f32[2,2,256,224]{3,2,0,1:T(8,128)S(1)} fusion(bf16[2,4096,256]{2,1,0:T(8,128)(2,1)} %get-tuple-element.21, bf16[2,2,224,4096]{3,2,1,0:T(8,128)(2,1)} %bitcast.99), kind=kOutput, calls=%fused_computation.13 | convolution fusion | flops 1879048192 | bytes 12451840 | tf_op jit(solution)/shard_map/qhrm,qmk->qhkr/dot_general | solution.py:125
  26.1 0.0 copy-start.3
  26.1 0.0 copy-done.2
  26.1 3.9 %fusion.13 = f32[2,256,224]{2,1,0:T(8,128)S(1)} fusion(bf16[2,4096,256]{2,1,0:T(8,128)(2,1)S(1)} %copy-done.2, f32[2,2,256,224]{3,2,0,1:T(8,128)S(1)} %fusion.7, bf16[2,2,224,4096]{3,2,1,0:T(8,128)(2,1)} %bitcast.100), kind=kOutput, calls=%fused_computation.15 | convolution fusion | flops 939753472 | bytes 9240576 | tf_op jit(solution)/shard_map/qrm,qmk->qkr/dot_general | solution.py:126
  30.1 4.1 %collective-permute-start = (f32[2,256,224]{2,1,0:T(8,128)S(1)}, f32[2,256,224]{2,1,0:T(8,128)S(1)}, u32[]{:S(2)}, u32[]{:S(2)}) collective-permute-start(f32[2,256,224]{2,1,0:T(8,128)S(1)} %fusion.13), channel_id=1, source_target_pairs={{0,32},{32,64},{64,96},{96,128},{128,160},{160,192},{192,224},{1,3... | collective-permute-start | bytes 1376264 | tf_op jit(solution)/shard_map/ppermute | solution.py:18
  34.2 0.0 copy-done.3
  34.2 0.0 copy-start.4
  34.3 6.3 %fusion.10 = f32[2,2,256,256]{3,2,1,0:T(8,128)S(1)} fusion(bf16[2,2,256,4096]{3,2,1,0:T(8,128)(2,1)} %bitcast.97, bf16[2,4096,256]{2,1,0:T(8,128)(2,1)S(1)} %copy-done.3), kind=kOutput, calls=%fused_computation.14 | convolution fusion | flops 2147483648 | bytes 13631488 | tf_op jit(solution)/shard_map/qhrm,qmk->qhkr/dot_general | solution.py:125
  40.6 0.0 copy-done.4
  40.6 0.1 copy.27
  40.7 0.1 copy.28
  40.8 0.1 copy.36
  40.9 5.2 %fusion.14 = f32[2,256,256]{2,1,0:T(8,128)S(1)} fusion(bf16[2,4096,256]{2,1,0:T(8,128)(2,1)} %get-tuple-element.22, bf16[2,2,256,4096]{3,2,1,0:T(8,128)(2,1)} %bitcast.98, f32[2,2,256,256]{3,2,1,0:T(8,128)S(1)} %fusion.10), kind=kOutput, calls=%fused_computation.16 | convolution fusion | flops 1074003968 | bytes 9961472 | tf_op jit(solution)/shard_map/qrm,qmk->qkr/dot_general | solution.py:126
  46.1 0.0 collective-permute-done
  46.1 0.1 slice_add_fusion.1
  46.2 2.2 %scatter-add.4 = f32[2,256,256]{2,1,0:T(8,128)S(1)} dynamic-update-slice(f32[2,256,256]{2,1,0:T(8,128)S(1)} %fusion.14, f32[2,256,224]{2,1,0:T(8,128)S(1)} %slice_add_fusion.1, s32[]{:T(128)} %constant.72.clone.1, s32[]{:T(128)} %constant.72.clone.1, s32[]{:T(128)} %constant.72.clone.1) | dynamic-update-slice | bytes 917508 | tf_op jit(solution)/shard_map/scatter-add | solution.py:147
  48.4 0.2 copy.35
  48.6 0.1 fusion.26
  48.7 0.2 copy.37
  48.9 0.2 convert_element_type.59
  49.1 0.5 broadcast.255
  49.6 2.2 %reduce.3 = bf16[256,512]{1,0:T(8,128)(2,1)S(1)} reduce(bf16[256,1,512]{2,1,0:T(2,128)(2,1)S(1)} %convert_element_type.59, bf16[]{:T(256)} %broadcast.255), dimensions={1}, to_apply=%convert_element_type.59.reduce_sub_computation | reduce | bytes 524290 | tf_op jit(solution)/shard_map/convert_element_type | solution.py:157
  51.9 0.1 reshape.305
  51.9 30.6 %all_to_all.6 = bf16[256,2,256]{2,1,0:T(2,128)(2,1)S(1)} all-to-all(bf16[256,2,256]{2,1,0:T(2,128)(2,1)S(1)} %reshape.305), channel_id=1, replica_groups=mesh['tm'=8,'stn'=32] {'tm','stn'}, dimensions={0} | all-to-all | bytes 524288 | tf_op jit(solution)/shard_map/all_to_all | solution.py:159
  82.5 0.2 reshape.306
  82.8 1.6 %reduce.2 = bf16[256,512]{1,0:T(8,128)(2,1)S(1)} reduce(bf16[256,1,512]{2,1,0:T(2,128)(2,1)S(1)} %reshape.306, bf16[]{:T(256)} %constant.84), dimensions={1}, to_apply=%all_to_all.4.reduce_sub_computation | reduce | bytes 524290 | tf_op jit(solution)/shard_map/all_to_all | solution.py:159
  84.3 0.6 reshape.300
  84.9 0.1 fusion.45
  85.1 0.3 copy.39
  85.4 0.1 copy.41
  85.4 0.5 neg.36
  86.0 0.1 copy.40
  86.1 0.5 squeeze.26
  86.6 1.1 %reshape_reshape.3 = bf16[128,1024]{1,0:T(8,128)(2,1)S(1)} reshape(bf16[2,8,8,32,32]{4,3,2,1,0:T(8,128)(2,1)S(1)} %copy.39) | data formatting | bytes 524288 | tf_op jit(solution)/shard_map/reshape;reshape | solution.py:163
  87.7 4.7 %convolution_multiply_fusion = f32[2048,1024]{1,0:T(8,128)} fusion(bf16[128,1024]{1,0:T(8,128)(2,1)S(1)} %reshape_reshape.3, bf16[64,1024]{1,0:T(8,128)(2,1)S(1)} %neg.36, bf16[64,1024]{1,0:T(8,128)(2,1)S(1)} %squeeze.26), kind=kOutput, calls=%fused_computation.4 | convolution fusion | flops 540540928 | bytes 8912896 | tf_op jit(solution)/shard_map/ki,kj->ij/dot_general | solution.py:165
  (5 shorter events, 0.1 us)
Async XLA Ops:
  2.6 5.2 %copy-start = (bf16[32,65536]{1,0:T(8,128)(2,1)S(1)}, bf16[32,65536]{1,0:T(8,128)(2,1)}, u32[]{:S(2)}) copy-start(bf16[32,65536]{1,0:T(8,128)(2,1)} %x_ref.1) | copy-start | bytes 12582916
  2.6 5.2 %copy-start.1 = (f32[8,8192]{1,0:T(8,128)S(1)}, f32[8,8192]{1,0:T(8,128)}, u32[]{:S(2)}) copy-start(f32[8,8192]{1,0:T(8,128)} %constant.83.clone.w_ref) | copy-start | bytes 786436
  18.7 7.4 %copy-start.2 = (bf16[2,4096,256]{2,1,0:T(8,128)(2,1)S(1)}, bf16[2,4096,256]{2,1,0:T(8,128)(2,1)}, u32[]{:S(2)}) copy-start(bf16[2,4096,256]{2,1,0:T(8,128)(2,1)} %get-tuple-element.22) | copy-start | bytes 12582916
  26.1 8.1 %copy-start.3 = (bf16[2,4096,256]{2,1,0:T(8,128)(2,1)S(1)}, bf16[2,4096,256]{2,1,0:T(8,128)(2,1)}, u32[]{:S(2)}) copy-start(bf16[2,4096,256]{2,1,0:T(8,128)(2,1)} %get-tuple-element.21) | copy-start | bytes 12582916
  30.1 16.0 %collective-permute-start = (f32[2,256,224]{2,1,0:T(8,128)S(1)}, f32[2,256,224]{2,1,0:T(8,128)S(1)}, u32[]{:S(2)}, u32[]{:S(2)}) collective-permute-start(f32[2,256,224]{2,1,0:T(8,128)S(1)} %fusion.13), channel_id=1, source_target_pairs={{0,32},{32,64},{64,96},{96,128},{128,160},{160,192},{192,224},{1,3... | collective-permute-start | bytes 1376264 | tf_op jit(solution)/shard_map/ppermute | solution.py:18
  34.2 6.3 %copy-start.4 = (f32[2,32,256]{2,1,0:T(8,128)S(1)}, f32[2,32,256]{2,1,0:T(8,128)}, u32[]{:S(2)}) copy-start(f32[2,32,256]{2,1,0:T(8,128)} %param.6) | copy-start | bytes 196612

commit v3 on v2

--- a/solution.py
+++ b/solution.py
@@ -1,3 +1,5 @@
+import functools
+
 import numpy as np
 
 import jax
@@ -37,31 +39,44 @@
 
 def band_tables(frame_len, band):
     half = band // 2
-    n_b = 32
+    n_b = 128
     n_a = frame_len // 2 // n_b
     q = jnp.arange(2, dtype=jnp.int32)[:, None, None]
-    k = jnp.arange(band, dtype=jnp.int32)[None, None, :]
+    k = jnp.arange(band, dtype=jnp.int32)[None, :, None]
     chan = 2 * (k % half) + q
-    imag_col = k >= half
-    a = jnp.arange(n_a, dtype=jnp.int32)[None, :, None]
-    b = jnp.arange(n_b, dtype=jnp.int32)[None, :, None]
-    p_steps = n_a * 2
+    imag_row = k >= half
+    a = jnp.arange(n_a, dtype=jnp.int32)[None, None, :]
+    b = jnp.arange(n_b, dtype=jnp.int32)[None, None, :]
+    p_steps = frame_len // n_b
     tp = (2.0 * jnp.pi / p_steps) * ((a * chan) % p_steps).astype(jnp.float32)
     tq = (2.0 * jnp.pi / frame_len) * ((b * (BAND_LOW + chan)) % frame_len).astype(jnp.float32)
     pr, pi = jnp.cos(tp), -jnp.sin(tp)
     qr, qi = jnp.cos(tq), -jnp.sin(tq)
-    b1 = jnp.where(imag_col, qi, qr)
-    b2 = jnp.where(imag_col, qr, -qi)
-    t = pr[:, :, None, :] * b1[:, None, :, :] + pi[:, :, None, :] * b2[:, None, :, :]
-    return split(t.reshape(2, n_a * n_b, band))
-
-
-def taps_kernel(x_ref, w_ref, own_ref, next_ref):
+    b1 = jnp.where(imag_row, qi, qr)
+    b2 = jnp.where(imag_row, qr, -qi)
+    t = pr[..., None] * b1[:, :, None, :] + pi[..., None] * b2[:, :, None, :]
+    return split(t.reshape(2, band, n_a * n_b))
+
+
+def taps_dft_kernel(x_ref, w_ref, th_hbm, tl_hbm, out_ref, lhs_ref, th_ref, tl_ref, sem, *, first_slot, n_slots):
+    step = pl.program_id(0)
+    steps = pl.num_programs(0)
+    block = x_ref.shape[0]
+    inputs = block * steps
     frame_len = w_ref.shape[1]
     half = frame_len // 2
     frames = x_ref.shape[1] // frame_len
     history = TAPS - 1
     lanes = 128
+    copy_hi = pltpu.make_async_copy(th_hbm, th_ref, sem.at[0])
+    copy_lo = pltpu.make_async_copy(tl_hbm, tl_ref, sem.at[1])
+
+    @pl.when(step == 0)
+    def _():
+        copy_hi.start()
+        copy_lo.start()
+
+    row0 = pl.multiple_of(step * block, block)
 
     def chunk(j, carry):
         base = pl.multiple_of(j * lanes, lanes)
@@ -70,7 +85,8 @@
         for offset in (0, half):
             xs.append([x_ref[:, pl.ds(f * frame_len + offset + base, lanes)].astype(jnp.float32) for f in range(frames)])
             ws.append([w_ref[pl.ds(p, 1), pl.ds(offset + base, lanes)] for p in range(TAPS)])
-        for s in range(frames + history):
+        for slot in range(n_slots):
+            s = first_slot + slot
             accs = []
             for part in range(2):
                 acc = None
@@ -81,50 +97,69 @@
                         acc = term if acc is None else acc + term
                 accs.append(acc)
             folded = (accs[0] + accs[1], accs[0] - accs[1])
-            ref, slot = (own_ref, s) if s < frames else (next_ref, s - frames)
+            rows = pl.ds(pl.multiple_of(slot * inputs + row0, block), block)
             for q in range(2):
                 hi = folded[q].astype(jnp.bfloat16)
                 lo = (folded[q] - hi.astype(jnp.float32)).astype(jnp.bfloat16)
-                ref[q, 0, slot, :, pl.ds(base, lanes)] = hi
-                ref[q, 1, slot, :, pl.ds(base, lanes)] = lo
+                lhs_ref[q, 0, rows, pl.ds(base, lanes)] = hi
+                lhs_ref[q, 1, rows, pl.ds(base, lanes)] = lo
         return carry
 
     lax.fori_loop(0, half // lanes, chunk, 0)
 
-
-def windowed_parts(voltages, window, frames):
+    @pl.when(step == steps - 1)
+    def _():
+        copy_hi.wait()
+        copy_lo.wait()
+        depth = 512
+        nt = (((1,), (1,)), ((), ()))
+        f32 = jnp.float32
+        for q in range(2):
+            out_ref[q] = jnp.zeros(out_ref.shape[1:], f32)
+
+            def kstep(kk, carry):
+                k0 = pl.multiple_of(kk * depth, depth)
+                cols = pl.ds(k0, depth)
+                hi = lhs_ref[q, 0, :, cols]
+                lo = lhs_ref[q, 1, :, cols]
+                t_hi = th_ref[q, :, cols]
+                t_lo = tl_ref[q, :, cols]
+                acc = lax.dot_general(t_hi, hi, nt, preferred_element_type=f32)
+                acc = acc + lax.dot_general(t_hi, lo, nt, preferred_element_type=f32)
+                acc = acc + lax.dot_general(t_lo, hi, nt, preferred_element_type=f32)
+                out_ref[q] += acc
+                return carry
+
+            lax.fori_loop(0, half // depth, kstep, 0)
+
+
+def band_spectra(voltages, window, t_hi, t_lo, frames, first_slot, n_slots):
     in_dev, length = voltages.shape
     frame_len = window.shape[1]
     half = frame_len // 2
-    history = TAPS - 1
+    band = t_hi.shape[1]
     block = 16
-    out_shape = (
-        jax.ShapeDtypeStruct((2, 2, frames, in_dev, half), jnp.bfloat16),
-        jax.ShapeDtypeStruct((2, 2, history, in_dev, half), jnp.bfloat16),
-    )
+    rows = n_slots * in_dev
+    kernel = functools.partial(taps_dft_kernel, first_slot=first_slot, n_slots=n_slots)
     return pl.pallas_call(
-        taps_kernel,
-        out_shape=out_shape,
+        kernel,
+        out_shape=jax.ShapeDtypeStruct((2, band, rows), jnp.float32),
         grid=(in_dev // block,),
         in_specs=[
             pl.BlockSpec((block, length), lambda g: (g, 0)),
             pl.BlockSpec((TAPS, frame_len), lambda g: (0, 0)),
+            pl.BlockSpec(memory_space=pl.ANY),
+            pl.BlockSpec(memory_space=pl.ANY),
         ],
-        out_specs=[
-            pl.BlockSpec((2, 2, frames, block, half), lambda g: (0, 0, 0, g, 0)),
-            pl.BlockSpec((2, 2, history, block, half), lambda g: (0, 0, 0, g, 0)),
+        out_specs=pl.BlockSpec((2, band, rows), lambda g: (0, 0, 0)),
+        scratch_shapes=[
+            pltpu.VMEM((2, 2, rows, half), jnp.bfloat16),
+            pltpu.VMEM((2, band, half), jnp.bfloat16),
+            pltpu.VMEM((2, band, half), jnp.bfloat16),
+            pltpu.SemaphoreType.DMA((2,)),
         ],
         compiler_params=pltpu.CompilerParams(vmem_limit_bytes=48 * 1024 * 1024),
-    )(voltages, window)
-
-
-def band_dft(parts, t_hi, t_lo):
-    q, h, slots, inputs, m = parts.shape
-    lhs = parts.reshape(q, h, slots * inputs, m)
-    f32 = jnp.float32
-    both = jnp.einsum("qhrm,qmk->qhkr", lhs, t_hi, preferred_element_type=f32)
-    high = jnp.einsum("qrm,qmk->qkr", lhs[:, 0], t_lo, preferred_element_type=f32)
-    return (both[:, 0] + both[:, 1]) + high
+    )(voltages, window, t_hi, t_lo)
 
 
 def on_device(voltages, gains):
@@ -140,10 +175,9 @@
     window = jnp.asarray(window_table(CHANNELS))
     t_hi, t_lo = band_tables(frame_len, band)
 
-    own_parts, next_parts = windowed_parts(voltages, window, frames)
-    raw_next = band_dft(next_parts, t_hi, t_lo)
+    raw_next = band_spectra(voltages, window, t_hi, t_lo, frames, frames, history)
     given = passed_along(raw_next, "tm", 1)
-    raw = band_dft(own_parts, t_hi, t_lo)
+    raw = band_spectra(voltages, window, t_hi, t_lo, frames, 0, frames)
     raw = raw.at[:, :, : history * in_dev].add(given)
 
     row = frames * in_dev

time: 92.5 us -> 102 us (1.10)
  matrix products: 27.5 us -> 4.67 us
  Pallas kernels: 10.9 us -> 24.2 us
  other arithmetic: 11.8 us -> 22 us
  local copies, waits for them, and re-layouts: 7.08 us -> 16.5 us
    dot_general x4 -> x0, matrix products: 22.9 us -> none  [the longest x2 13.7 us: band_dft(): both = jnp.einsum('qhrm,qmk->qhkr', lhs, t_hi, preferred_element_type=f32)]
    pallas_call x1 -> x2, Pallas kernels: 10.9 us -> 24.2 us  [band_spectra(): pl.pallas_call(kernel, out_shape=jax.ShapeDtypeStruct((2, band, rows), jn...]
    add x0 -> x1, local copies, waits for them, and re-layouts: none -> 9.39 us  [band_tables(): t = pr[..., None] * b1[:, :, None, :] + pi[..., None] * b2[:, :, None, :]]
    add x1, other arithmetic: 1.23 us -> 6.94 us  [band_tables(): t = pr[..., None] * b1[:, :, None, :] + pi[..., None] * b2[:, :, None, :]]
    convert_element_type x1, other arithmetic: 5.16 us -> 8.67 us  [split(): return (hi.astype(jnp.bfloat16), lo.astype(jnp.bfloat16))]
  transfers between devices with their start and end apart: 1 -> 1, of which waited for: 0 -> 0; matrix products, arithmetic and copies ran while one was open for 13% -> 0% of each run, Pallas kernels for 0% -> 12%
where the time goes in v3:
time: 102 us
  blocking collectives  30.3 us (30%)
  Pallas kernels  24.2 us (24%)
  other arithmetic  22 us (22%)
  local copies, waits for them, and re-layouts  16.5 us (16%)
  matrix products  4.67 us (5%)
  starting transfers between devices  4.1 us (4%)
    all_to_all x1, blocking collectives, on_device(): lax.all_to_all(spectra, ('tm', 'stn'), split_axis=0, concat_axis=0, tiled...  30.3 us
    pallas_call x2, Pallas kernels, band_spectra(): pl.pallas_call(kernel, out_shape=jax.ShapeDtypeStruct((2, band, rows), jn...  24.2 us
    add x1, local copies, waits for them, and re-layouts, band_tables(): t = pr[..., None] * b1[:, :, None, :] + pi[..., None] * b2[:, :, None, :]  9.39 us
    convert_element_type x1, other arithmetic, split(): return (hi.astype(jnp.bfloat16), lo.astype(jnp.bfloat16))  8.67 us
    add x1, other arithmetic, band_tables(): t = pr[..., None] * b1[:, :, None, :] + pi[..., None] * b2[:, :, None, :]  6.94 us
    dot_general x1, matrix products, on_device(): jnp.einsum('ki,kj->ij', both, stacked, preferred_element_type=jnp.float32)  4.67 us
    ppermute x1, starting transfers between devices, passed_along(): return lax.ppermute(x, axis, pairs)  4.1 us
    convert_element_type x1, other arithmetic, on_device(): spectra = jnp.stack([spec_re, spec_im], axis=2).astype(jnp.bfloat16)  2.21 us
  transfers between devices with their start and end apart: 1, of which 0 were waited for; matrix products, arithmetic and copies ran while one was open for 0% of the time, Pallas kernels for 12%

profile of v3, /device:TPU:1, one launch (start us, length us, event | category | flops | bytes accessed | tf_op | source)
XLA Modules:
  0.0 101.9 jit_solution(17222610640701620291)
XLA Ops:
  0.0 1.1 %fusion.25 = (f32[2,256,32]{2,1,0:T(8,128)S(1)}, f32[2,256,32]{2,1,0:T(8,128)S(1)}) fusion(s32[2,256]{1,0:T(2,128)S(1)} %get-tuple-element.29), kind=kLoop, calls=%fused_computation.48 | loop fusion | flops 245760 | bytes 133120 | tf_op jit(solution)/shard_map/cos | solution.py:53
  1.1 1.1 %negate_select_fusion.4 = (f32[2,256,128]{2,1,0:T(8,128)S(1)}, f32[2,256,128]{2,1,0:T(8,128)S(1)}) fusion(s32[2,256]{1,0:T(2,128)S(1)} %get-tuple-element.30, pred[256]{0:T(512)(128)(4,1)S(1)} %iota_compare_fusion), kind=kLoop, calls=%fused_computation.36 | loop fusion | flops 1114112 | bytes 526592 | tf_op jit(solution)/shard_map/jit(_where)/select_n | solution.py:55
  2.3 6.9 %multiply_add_fusion = f32[2,256,32,128]{3,2,1,0:T(8,128)} fusion(f32[2,256,128]{2,1,0:T(8,128)S(1)} %get-tuple-element.26, f32[2,256,32]{2,1,0:T(8,128)S(1)} %get-tuple-element.28, f32[2,256,128]{2,1,0:T(8,128)S(1)} %get-tuple-element.25, f32[2,256,32]{2,1,0:T(8,128)S(1)} %get-tuple-element.27), kind=kLoop, calls=%fused_computation.3 | loop fusion | flops 6291456 | bytes 9043968 | tf_op jit(solution)/shard_map/add | solution.py:57
  9.2 9.4 %add.156 = f32[2,256,4096]{2,1,0:T(8,128)} reshape(f32[2,256,32,128]{3,2,1,0:T(8,128)} %multiply_add_fusion) | data formatting | bytes 16777216 | tf_op jit(solution)/shard_map/add | solution.py:57
  18.6 0.0 copy-start
  18.6 0.0 copy-start.1
  18.6 8.7 %fusion = (bf16[2,256,4096]{2,1,0:T(8,128)(2,1)}, bf16[2,256,4096]{2,1,0:T(8,128)(2,1)}) fusion(f32[2,256,4096]{2,1,0:T(8,128)} %add.156), kind=kLoop, calls=%fused_computation.2 | loop fusion | flops 8388608 | bytes 16777216 | tf_op jit(solution)/shard_map/convert_element_type | solution.py:37
  27.3 0.0 copy-done
  27.3 0.0 copy-done.1
  27.3 11.8 %shard_map.38 = f32[2,256,224]{2,1,0:T(8,128)S(1)} custom-call(bf16[32,65536]{1,0:T(8,128)(2,1)S(1)} %copy-done, f32[8,8192]{1,0:T(8,128)S(1)} %copy-done.1, bf16[2,256,4096]{2,1,0:T(8,128)(2,1)} %get-tuple-element.18.th_hbm, bf16[2,256,4096]{2,1,0:T(8,128)(2,1)} %get-tuple-element.17.tl_hbm), custom_call_target="tpu_custom_call" | custom-call | tf_op jit(solution)/shard_map/pallas_call | solution.py:144
  39.1 0.0 copy-start.2
  39.1 4.1 %collective-permute-start = (f32[2,256,224]{2,1,0:T(8,128)S(1)}, f32[2,256,224]{2,1,0:T(8,128)S(1)}, u32[]{:S(2)}, u32[]{:S(2)}) collective-permute-start(f32[2,256,224]{2,1,0:T(8,128)S(1)} %shard_map.38), channel_id=1, source_target_pairs={{0,32},{32,64},{64,96},{96,128},{128,160},{160,192},{192,224},{1,3... | collective-permute-start | bytes 1376264 | tf_op jit(solution)/shard_map/ppermute | solution.py:20
  43.2 12.4 %shard_map.37 = f32[2,256,256]{2,1,0:T(8,128)S(1)} custom-call(bf16[32,65536]{1,0:T(8,128)(2,1)S(1)} %copy-done, f32[8,8192]{1,0:T(8,128)S(1)} %copy-done.1, bf16[2,256,4096]{2,1,0:T(8,128)(2,1)} %get-tuple-element.18.th_hbm, bf16[2,256,4096]{2,1,0:T(8,128)(2,1)} %get-tuple-element.17.tl_hbm), custom_call_target="tpu_custom_call" | custom-call | tf_op jit(solution)/shard_map/pallas_call | solution.py:144
  55.7 0.0 copy-done.2
  55.7 0.1 copy.15
  55.8 0.1 copy.16
  55.9 0.1 copy.18
  56.0 0.0 collective-permute-done
  56.0 0.1 slice_add_fusion
  56.1 2.2 %scatter-add.4 = f32[2,256,256]{2,1,0:T(8,128)S(1)} dynamic-update-slice(f32[2,256,256]{2,1,0:T(8,128)S(1)} %shard_map.37, f32[2,256,224]{2,1,0:T(8,128)S(1)} %slice_add_fusion, s32[]{:T(128)} %constant.72.clone.1, s32[]{:T(128)} %constant.72.clone.1, s32[]{:T(128)} %constant.72.clone.1) | dynamic-update-slice | bytes 917508 | tf_op jit(solution)/shard_map/scatter-add | solution.py:181
  58.2 0.2 copy.17
  58.4 0.1 fusion.13
  58.6 0.2 copy.19
  58.7 0.2 convert_element_type.59
  59.0 0.5 broadcast.257
  59.5 2.2 %reduce.3 = bf16[256,512]{1,0:T(8,128)(2,1)S(1)} reduce(bf16[256,1,512]{2,1,0:T(2,128)(2,1)S(1)} %convert_element_type.59, bf16[]{:T(256)} %broadcast.257), dimensions={1}, to_apply=%convert_element_type.59.reduce_sub_computation | reduce | bytes 524290 | tf_op jit(solution)/shard_map/convert_element_type | solution.py:191
  61.7 0.1 reshape.295
  61.8 30.3 %all_to_all.6 = bf16[256,2,256]{2,1,0:T(2,128)(2,1)S(1)} all-to-all(bf16[256,2,256]{2,1,0:T(2,128)(2,1)S(1)} %reshape.295), channel_id=1, replica_groups=mesh['tm'=8,'stn'=32] {'tm','stn'}, dimensions={0} | all-to-all | bytes 524288 | tf_op jit(solution)/shard_map/all_to_all | solution.py:193
  92.0 0.2 reshape.296
  92.3 1.6 %reduce.2 = bf16[256,512]{1,0:T(8,128)(2,1)S(1)} reduce(bf16[256,1,512]{2,1,0:T(2,128)(2,1)S(1)} %reshape.296, bf16[]{:T(256)} %constant.84), dimensions={1}, to_apply=%all_to_all.4.reduce_sub_computation | reduce | bytes 524290 | tf_op jit(solution)/shard_map/all_to_all | solution.py:193
  93.8 0.6 reshape.292
  94.4 0.1 fusion.28
  94.6 0.3 copy.21
  94.9 0.1 copy.23
  95.0 0.5 neg.36
  95.5 0.1 copy.22
  95.6 0.5 squeeze.14
  96.1 1.1 %reshape_reshape.3 = bf16[128,1024]{1,0:T(8,128)(2,1)S(1)} reshape(bf16[2,8,8,32,32]{4,3,2,1,0:T(8,128)(2,1)S(1)} %copy.21) | data formatting | bytes 524288 | tf_op jit(solution)/shard_map/reshape;reshape | solution.py:197
  97.2 4.7 %convolution_multiply_fusion = f32[2048,1024]{1,0:T(8,128)} fusion(bf16[128,1024]{1,0:T(8,128)(2,1)S(1)} %reshape_reshape.3, bf16[64,1024]{1,0:T(8,128)(2,1)S(1)} %neg.36, bf16[64,1024]{1,0:T(8,128)(2,1)S(1)} %squeeze.14), kind=kOutput, calls=%fused_computation.4 | convolution fusion | flops 540540928 | bytes 8912896 | tf_op jit(solution)/shard_map/ki,kj->ij/dot_general | solution.py:199
  (5 shorter events, 0.1 us)
Async XLA Ops:
  18.6 8.7 %copy-start = (bf16[32,65536]{1,0:T(8,128)(2,1)S(1)}, bf16[32,65536]{1,0:T(8,128)(2,1)}, u32[]{:S(2)}) copy-start(bf16[32,65536]{1,0:T(8,128)(2,1)} %x_ref.3) | copy-start | bytes 12582916
  18.6 8.7 %copy-start.1 = (f32[8,8192]{1,0:T(8,128)S(1)}, f32[8,8192]{1,0:T(8,128)}, u32[]{:S(2)}) copy-start(f32[8,8192]{1,0:T(8,128)} %constant.83.clone.w_ref) | copy-start | bytes 786436
  39.1 16.6 %copy-start.2 = (f32[2,32,256]{2,1,0:T(8,128)S(1)}, f32[2,32,256]{2,1,0:T(8,128)}, u32[]{:S(2)}) copy-start(f32[2,32,256]{2,1,0:T(8,128)} %param.6) | copy-start | bytes 196612
  39.1 16.9 %collective-permute-start = (f32[2,256,224]{2,1,0:T(8,128)S(1)}, f32[2,256,224]{2,1,0:T(8,128)S(1)}, u32[]{:S(2)}, u32[]{:S(2)}) collective-permute-start(f32[2,256,224]{2,1,0:T(8,128)S(1)} %shard_map.38), channel_id=1, source_target_pairs={{0,32},{32,64},{64,96},{96,128},{128,160},{160,192},{192,224},{1,3... | collective-permute-start | bytes 1376264 | tf_op jit(solution)/shard_map/ppermute | solution.py:20

commit v4 on v3

--- a/solution.py
+++ b/solution.py
@@ -39,23 +39,23 @@
 
 def band_tables(frame_len, band):
     half = band // 2
-    n_b = 128
+    n_b = 32
     n_a = frame_len // 2 // n_b
     q = jnp.arange(2, dtype=jnp.int32)[:, None, None]
-    k = jnp.arange(band, dtype=jnp.int32)[None, :, None]
+    k = jnp.arange(band, dtype=jnp.int32)[None, None, :]
     chan = 2 * (k % half) + q
-    imag_row = k >= half
-    a = jnp.arange(n_a, dtype=jnp.int32)[None, None, :]
-    b = jnp.arange(n_b, dtype=jnp.int32)[None, None, :]
-    p_steps = frame_len // n_b
+    imag_col = k >= half
+    a = jnp.arange(n_a, dtype=jnp.int32)[None, :, None]
+    b = jnp.arange(n_b, dtype=jnp.int32)[None, :, None]
+    p_steps = n_a * 2
     tp = (2.0 * jnp.pi / p_steps) * ((a * chan) % p_steps).astype(jnp.float32)
     tq = (2.0 * jnp.pi / frame_len) * ((b * (BAND_LOW + chan)) % frame_len).astype(jnp.float32)
     pr, pi = jnp.cos(tp), -jnp.sin(tp)
     qr, qi = jnp.cos(tq), -jnp.sin(tq)
-    b1 = jnp.where(imag_row, qi, qr)
-    b2 = jnp.where(imag_row, qr, -qi)
-    t = pr[..., None] * b1[:, :, None, :] + pi[..., None] * b2[:, :, None, :]
-    return split(t.reshape(2, band, n_a * n_b))
+    b1 = jnp.where(imag_col, qi, qr)
+    b2 = jnp.where(imag_col, qr, -qi)
+    t = pr[:, :, None, :] * b1[:, None, :, :] + pi[:, :, None, :] * b2[:, None, :, :]
+    return split(t.reshape(2, n_a * n_b, band))
 
 
 def taps_dft_kernel(x_ref, w_ref, th_hbm, tl_hbm, out_ref, lhs_ref, th_ref, tl_ref, sem, *, first_slot, n_slots):
@@ -112,7 +112,6 @@
         copy_hi.wait()
         copy_lo.wait()
         depth = 512
-        nt = (((1,), (1,)), ((), ()))
         f32 = jnp.float32
         for q in range(2):
             out_ref[q] = jnp.zeros(out_ref.shape[1:], f32)
@@ -122,11 +121,11 @@
                 cols = pl.ds(k0, depth)
                 hi = lhs_ref[q, 0, :, cols]
                 lo = lhs_ref[q, 1, :, cols]
-                t_hi = th_ref[q, :, cols]
-                t_lo = tl_ref[q, :, cols]
-                acc = lax.dot_general(t_hi, hi, nt, preferred_element_type=f32)
-                acc = acc + lax.dot_general(t_hi, lo, nt, preferred_element_type=f32)
-                acc = acc + lax.dot_general(t_lo, hi, nt, preferred_element_type=f32)
+                t_hi = th_ref[q, cols, :]
+                t_lo = tl_ref[q, cols, :]
+                acc = jnp.dot(hi, t_hi, preferred_element_type=f32)
+                acc = acc + jnp.dot(lo, t_hi, preferred_element_type=f32)
+                acc = acc + jnp.dot(hi, t_lo, preferred_element_type=f32)
                 out_ref[q] += acc
                 return carry
 
@@ -137,13 +136,13 @@
     in_dev, length = voltages.shape
     frame_len = window.shape[1]
     half = frame_len // 2
-    band = t_hi.shape[1]
+    band = t_hi.shape[2]
     block = 16
     rows = n_slots * in_dev
     kernel = functools.partial(taps_dft_kernel, first_slot=first_slot, n_slots=n_slots)
     return pl.pallas_call(
         kernel,
-        out_shape=jax.ShapeDtypeStruct((2, band, rows), jnp.float32),
+        out_shape=jax.ShapeDtypeStruct((2, rows, band), jnp.float32),
         grid=(in_dev // block,),
         in_specs=[
             pl.BlockSpec((block, length), lambda g: (g, 0)),
@@ -151,11 +150,11 @@
             pl.BlockSpec(memory_space=pl.ANY),
             pl.BlockSpec(memory_space=pl.ANY),
         ],
-        out_specs=pl.BlockSpec((2, band, rows), lambda g: (0, 0, 0)),
+        out_specs=pl.BlockSpec((2, rows, band), lambda g: (0, 0, 0)),
         scratch_shapes=[
             pltpu.VMEM((2, 2, rows, half), jnp.bfloat16),
-            pltpu.VMEM((2, band, half), jnp.bfloat16),
-            pltpu.VMEM((2, band, half), jnp.bfloat16),
+            pltpu.VMEM((2, half, band), jnp.bfloat16),
+            pltpu.VMEM((2, half, band), jnp.bfloat16),
             pltpu.SemaphoreType.DMA((2,)),
         ],
         compiler_params=pltpu.CompilerParams(vmem_limit_bytes=48 * 1024 * 1024),
@@ -178,7 +177,8 @@
     raw_next = band_spectra(voltages, window, t_hi, t_lo, frames, frames, history)
     given = passed_along(raw_next, "tm", 1)
     raw = band_spectra(voltages, window, t_hi, t_lo, frames, 0, frames)
-    raw = raw.at[:, :, : history * in_dev].add(given)
+    raw = raw.at[:, : history * in_dev, :].add(given)
+    raw = jnp.transpose(raw, (0, 2, 1))
 
     row = frames * in_dev
     raw = jnp.transpose(raw.reshape(2, 2, half_band, row), (1, 2, 0, 3))

time: 102 us -> 79.1 us (0.78)
  local copies, waits for them, and re-layouts: 16.5 us -> 4.76 us
  other arithmetic: 22 us -> 12 us
  Pallas kernels: 24.2 us -> 23 us
    add x1 -> x0, local copies, waits for them, and re-layouts: 9.39 us -> none  [band_tables(): t = pr[..., None] * b1[:, :, None, :] + pi[..., None] * b2[:, :, None, :]]
    add x2 -> x1, other arithmetic: 7.03 us -> 1.23 us  [band_tables(): pr[:, :, None, :] * b1[:, None, :, :]]
    convert_element_type x1, other arithmetic: 8.67 us -> 5.24 us  [split(): return (hi.astype(jnp.bfloat16), lo.astype(jnp.bfloat16))]
    scatter-add x1 -> x0, local copies, waits for them, and re-layouts: 2.16 us -> none  [on_device(): raw = raw.at[:, :, :history * in_dev].add(given)]
    pallas_call x2, Pallas kernels: 24.2 us -> 23 us  [band_spectra(): pl.pallas_call(kernel, out_shape=jax.ShapeDtypeStruct((2, rows, band), jn...]
  transfers between devices with their start and end apart: 1 -> 1, of which waited for: 0 -> 0; matrix products, arithmetic and copies ran while one was open for 0% -> 0% of each run, Pallas kernels for 12% -> 15%
where the time goes in v4:
time: 79.1 us; the launch traced here: 79 us
  blocking collectives  30.2 us (38%)
  Pallas kernels  23 us (29%)
  other arithmetic  12 us (15%)
  local copies, waits for them, and re-layouts  4.76 us (6%)
  matrix products  4.68 us (6%)
  starting transfers between devices  4.1 us (5%)
    all_to_all x1, blocking collectives, on_device(): lax.all_to_all(spectra, ('tm', 'stn'), split_axis=0, concat_axis=0, tiled...  30.2 us
    pallas_call x2, Pallas kernels, band_spectra(): pl.pallas_call(kernel, out_shape=jax.ShapeDtypeStruct((2, rows, band), jn...  23 us
    convert_element_type x1, other arithmetic, split(): return (hi.astype(jnp.bfloat16), lo.astype(jnp.bfloat16))  5.24 us
    dot_general x1, matrix products, on_device(): jnp.einsum('ki,kj->ij', both, stacked, preferred_element_type=jnp.float32)  4.68 us
    ppermute x1, starting transfers between devices, passed_along(): return lax.ppermute(x, axis, pairs)  4.1 us
    convert_element_type x1, other arithmetic, on_device(): spectra = jnp.stack([spec_re, spec_im], axis=2).astype(jnp.bfloat16)  2.21 us
  transfers between devices with their start and end apart: 1, of which 0 were waited for; matrix products, arithmetic and copies ran while one was open for 0% of the time, Pallas kernels for 15%

profile of v4, /device:TPU:1, one launch (start us, length us, event | category | flops | bytes accessed | tf_op | source)
XLA Modules:
  0.0 79.0 jit_solution(9544222111190886642)
XLA Ops:
  0.0 1.0 %fusion.17 = (f32[2,128,256]{2,1,0:T(8,128)S(1)}, f32[2,128,256]{2,1,0:T(8,128)S(1)}) fusion(s32[2,256]{1,0:T(2,128)S(1)} %get-tuple-element.29), kind=kLoop, calls=%fused_computation.37 | loop fusion | flops 983040 | bytes 526336 | tf_op jit(solution)/shard_map/cos | solution.py:53
  1.1 0.3 negate_select_fusion.4
  1.4 1.2 %multiply_add_fusion = f32[2,128,32,256]{3,2,1,0:T(8,128)S(1)} fusion(f32[2,32,256]{2,1,0:T(8,128)S(1)} %get-tuple-element.26, f32[2,128,256]{2,1,0:T(8,128)S(1)} %get-tuple-element.28, f32[2,32,256]{2,1,0:T(8,128)S(1)} %get-tuple-element.25, f32[2,128,256]{2,1,0:T(8,128)S(1)} %get-tuple-element.27), kind=kLoop, calls=%fused_computation.3 | loop fusion | flops 6291456 | bytes 9043968 | tf_op jit(solution)/shard_map/add | solution.py:57
  2.6 0.0 copy-start
  2.6 0.0 copy-start.1
  2.6 5.2 %fusion = (bf16[2,4096,256]{2,1,0:T(8,128)(2,1)}, bf16[2,4096,256]{2,1,0:T(8,128)(2,1)}) fusion(f32[2,128,32,256]{3,2,1,0:T(8,128)S(1)} %multiply_add_fusion), kind=kLoop, calls=%fused_computation.2 | loop fusion | flops 8388608 | bytes 16777216 | tf_op jit(solution)/shard_map/convert_element_type | solution.py:37
  7.9 0.0 copy-done
  7.9 0.0 copy-done.1
  7.9 11.0 %shard_map.38 = f32[2,224,256]{2,1,0:T(8,128)S(1)} custom-call(bf16[32,65536]{1,0:T(8,128)(2,1)S(1)} %copy-done, f32[8,8192]{1,0:T(8,128)S(1)} %copy-done.1, bf16[2,4096,256]{2,1,0:T(8,128)(2,1)} %get-tuple-element.18.th_hbm, bf16[2,4096,256]{2,1,0:T(8,128)(2,1)} %get-tuple-element.17.tl_hbm), custom_call_target="tpu_custom_call" | custom-call | tf_op jit(solution)/shard_map/pallas_call | solution.py:143
  18.9 0.0 copy-start.2
  18.9 4.1 %collective-permute-start = (f32[2,224,256]{2,1,0:T(8,128)S(1)}, f32[2,224,256]{2,1,0:T(8,128)S(1)}, u32[]{:S(2)}, u32[]{:S(2)}) collective-permute-start(f32[2,224,256]{2,1,0:T(8,128)S(1)} %shard_map.38), channel_id=1, source_target_pairs={{0,32},{32,64},{64,96},{96,128},{128,160},{160,192},{192,224},{1,3... | collective-permute-start | bytes 1376264 | tf_op jit(solution)/shard_map/ppermute | solution.py:20
  23.0 12.0 %shard_map.37 = f32[2,256,256]{2,1,0:T(8,128)S(1)} custom-call(bf16[32,65536]{1,0:T(8,128)(2,1)S(1)} %copy-done, f32[8,8192]{1,0:T(8,128)S(1)} %copy-done.1, bf16[2,4096,256]{2,1,0:T(8,128)(2,1)} %get-tuple-element.18.th_hbm, bf16[2,4096,256]{2,1,0:T(8,128)(2,1)} %get-tuple-element.17.tl_hbm), custom_call_target="tpu_custom_call" | custom-call | tf_op jit(solution)/shard_map/pallas_call | solution.py:143
  35.0 0.0 copy-done.2
  35.0 0.1 copy.20
  35.2 0.1 copy.21
  35.2 0.1 copy.23
  35.3 0.0 collective-permute-done
  35.3 0.1 fusion.6
  35.5 0.1 fusion.11
  35.6 0.2 copy.24
  35.8 0.2 convert_element_type.59
  36.0 0.5 broadcast.255
  36.6 2.2 %reduce.3 = bf16[256,512]{1,0:T(8,128)(2,1)S(1)} reduce(bf16[256,1,512]{2,1,0:T(2,128)(2,1)S(1)} %convert_element_type.59, bf16[]{:T(256)} %broadcast.255), dimensions={1}, to_apply=%convert_element_type.59.reduce_sub_computation | reduce | bytes 524290 | tf_op jit(solution)/shard_map/convert_element_type | solution.py:191
  38.8 0.1 reshape.293
  38.8 30.2 %all_to_all.6 = bf16[256,2,256]{2,1,0:T(2,128)(2,1)S(1)} all-to-all(bf16[256,2,256]{2,1,0:T(2,128)(2,1)S(1)} %reshape.293), channel_id=1, replica_groups=mesh['tm'=8,'stn'=32] {'tm','stn'}, dimensions={0} | all-to-all | bytes 524288 | tf_op jit(solution)/shard_map/all_to_all | solution.py:193
  69.1 0.2 reshape.294
  69.3 1.6 %reduce.2 = bf16[256,512]{1,0:T(8,128)(2,1)S(1)} reduce(bf16[256,1,512]{2,1,0:T(2,128)(2,1)S(1)} %reshape.294, bf16[]{:T(256)} %constant.84), dimensions={1}, to_apply=%all_to_all.4.reduce_sub_computation | reduce | bytes 524290 | tf_op jit(solution)/shard_map/all_to_all | solution.py:193
  70.9 0.6 reshape.290
  71.5 0.1 fusion.29
  71.6 0.3 copy.26
  71.9 0.1 copy.28
  72.0 0.5 neg.36
  72.5 0.1 copy.27
  72.6 0.5 squeeze.14
  73.2 1.1 %reshape_reshape.3 = bf16[128,1024]{1,0:T(8,128)(2,1)S(1)} reshape(bf16[2,8,8,32,32]{4,3,2,1,0:T(8,128)(2,1)S(1)} %copy.26) | data formatting | bytes 524288 | tf_op jit(solution)/shard_map/reshape;reshape | solution.py:197
  74.3 4.7 %convolution_multiply_fusion = f32[2048,1024]{1,0:T(8,128)} fusion(bf16[128,1024]{1,0:T(8,128)(2,1)S(1)} %reshape_reshape.3, bf16[64,1024]{1,0:T(8,128)(2,1)S(1)} %neg.36, bf16[64,1024]{1,0:T(8,128)(2,1)S(1)} %squeeze.14), kind=kOutput, calls=%fused_computation.4 | convolution fusion | flops 540540928 | bytes 8912896 | tf_op jit(solution)/shard_map/ki,kj->ij/dot_general | solution.py:199
  (6 shorter events, 0.1 us)
Async XLA Ops:
  2.6 5.3 %copy-start = (bf16[32,65536]{1,0:T(8,128)(2,1)S(1)}, bf16[32,65536]{1,0:T(8,128)(2,1)}, u32[]{:S(2)}) copy-start(bf16[32,65536]{1,0:T(8,128)(2,1)} %x_ref.3) | copy-start | bytes 12582916
  2.6 5.3 %copy-start.1 = (f32[8,8192]{1,0:T(8,128)S(1)}, f32[8,8192]{1,0:T(8,128)}, u32[]{:S(2)}) copy-start(f32[8,8192]{1,0:T(8,128)} %constant.83.clone.w_ref) | copy-start | bytes 786436
  18.9 16.1 %copy-start.2 = (f32[2,32,256]{2,1,0:T(8,128)S(1)}, f32[2,32,256]{2,1,0:T(8,128)}, u32[]{:S(2)}) copy-start(f32[2,32,256]{2,1,0:T(8,128)} %param.6) | copy-start | bytes 196612
  18.9 16.4 %collective-permute-start = (f32[2,224,256]{2,1,0:T(8,128)S(1)}, f32[2,224,256]{2,1,0:T(8,128)S(1)}, u32[]{:S(2)}, u32[]{:S(2)}) collective-permute-start(f32[2,224,256]{2,1,0:T(8,128)S(1)} %shard_map.38), channel_id=1, source_target_pairs={{0,32},{32,64},{64,96},{96,128},{128,160},{160,192},{192,224},{1,3... | collective-permute-start | bytes 1376264 | tf_op jit(solution)/shard_map/ppermute | solution.py:20

commit v5 on v4

--- a/solution.py
+++ b/solution.py
@@ -55,10 +55,12 @@
     b1 = jnp.where(imag_col, qi, qr)
     b2 = jnp.where(imag_col, qr, -qi)
     t = pr[:, :, None, :] * b1[:, None, :, :] + pi[:, :, None, :] * b2[:, None, :, :]
-    return split(t.reshape(2, n_a * n_b, band))
-
-
-def taps_dft_kernel(x_ref, w_ref, th_hbm, tl_hbm, out_ref, lhs_ref, th_ref, tl_ref, sem, *, first_slot, n_slots):
+    t = t.reshape(2, n_a * n_b, band)
+    hi = lax.reduce_precision(t, exponent_bits=8, mantissa_bits=7)
+    return jnp.stack([hi, t - hi]).astype(jnp.bfloat16)
+
+
+def taps_dft_kernel(x_ref, w_ref, table_hbm, out_ref, lhs_ref, th_ref, tl_ref, sem, *, first_slot, n_slots):
     step = pl.program_id(0)
     steps = pl.num_programs(0)
     block = x_ref.shape[0]
@@ -68,8 +70,8 @@
     frames = x_ref.shape[1] // frame_len
     history = TAPS - 1
     lanes = 128
-    copy_hi = pltpu.make_async_copy(th_hbm, th_ref, sem.at[0])
-    copy_lo = pltpu.make_async_copy(tl_hbm, tl_ref, sem.at[1])
+    copy_hi = pltpu.make_async_copy(table_hbm.at[0], th_ref, sem.at[0])
+    copy_lo = pltpu.make_async_copy(table_hbm.at[1], tl_ref, sem.at[1])
 
     @pl.when(step == 0)
     def _():
@@ -119,24 +121,24 @@
             def kstep(kk, carry):
                 k0 = pl.multiple_of(kk * depth, depth)
                 cols = pl.ds(k0, depth)
-                hi = lhs_ref[q, 0, :, cols]
-                lo = lhs_ref[q, 1, :, cols]
+                rows = lhs_ref.shape[2]
+                both = lhs_ref[q, :, :, cols].reshape(2 * rows, depth)
                 t_hi = th_ref[q, cols, :]
                 t_lo = tl_ref[q, cols, :]
-                acc = jnp.dot(hi, t_hi, preferred_element_type=f32)
-                acc = acc + jnp.dot(lo, t_hi, preferred_element_type=f32)
-                acc = acc + jnp.dot(hi, t_lo, preferred_element_type=f32)
+                acc = jnp.dot(both, t_hi, preferred_element_type=f32)
+                acc = acc[:rows] + acc[rows:]
+                acc = acc + jnp.dot(both[:rows], t_lo, preferred_element_type=f32)
                 out_ref[q] += acc
                 return carry
 
             lax.fori_loop(0, half // depth, kstep, 0)
 
 
-def band_spectra(voltages, window, t_hi, t_lo, frames, first_slot, n_slots):
+def band_spectra(voltages, window, table, frames, first_slot, n_slots):
     in_dev, length = voltages.shape
     frame_len = window.shape[1]
     half = frame_len // 2
-    band = t_hi.shape[2]
+    band = table.shape[3]
     block = 16
     rows = n_slots * in_dev
     kernel = functools.partial(taps_dft_kernel, first_slot=first_slot, n_slots=n_slots)
@@ -148,7 +150,6 @@
             pl.BlockSpec((block, length), lambda g: (g, 0)),
             pl.BlockSpec((TAPS, frame_len), lambda g: (0, 0)),
             pl.BlockSpec(memory_space=pl.ANY),
-            pl.BlockSpec(memory_space=pl.ANY),
         ],
         out_specs=pl.BlockSpec((2, rows, band), lambda g: (0, 0, 0)),
         scratch_shapes=[
@@ -158,7 +159,7 @@
             pltpu.SemaphoreType.DMA((2,)),
         ],
         compiler_params=pltpu.CompilerParams(vmem_limit_bytes=48 * 1024 * 1024),
-    )(voltages, window, t_hi, t_lo)
+    )(voltages, window, table)
 
 
 def on_device(voltages, gains):
@@ -172,11 +173,11 @@
     all_inputs = in_dev * n_station
     history = TAPS - 1
     window = jnp.asarray(window_table(CHANNELS))
-    t_hi, t_lo = band_tables(frame_len, band)
-
-    raw_next = band_spectra(voltages, window, t_hi, t_lo, frames, frames, history)
+    table = band_tables(frame_len, band)
+
+    raw_next = band_spectra(voltages, window, table, frames, frames, history)
     given = passed_along(raw_next, "tm", 1)
-    raw = band_spectra(voltages, window, t_hi, t_lo, frames, 0, frames)
+    raw = band_spectra(voltages, window, table, frames, 0, frames)
     raw = raw.at[:, : history * in_dev, :].add(given)
     raw = jnp.transpose(raw, (0, 2, 1))
 

time: 79.1 us -> 86.2 us (1.090)
  other arithmetic: 12 us -> 19 us
    another operation x1 -> x3, other arithmetic: 0.07 us -> 12.4 us  [the longest x1 7.76 us: band_tables(): return jnp.stack([hi, t - hi]).astype(jnp.bfloat16)]
    convert_element_type x1 -> x0, other arithmetic: 5.24 us -> none  [split(): return (hi.astype(jnp.bfloat16), lo.astype(jnp.bfloat16))]
  transfers between devices with their start and end apart: 1 -> 1, of which waited for: 0 -> 0; matrix products, arithmetic and copies ran while one was open for 0% -> 0% of each run, Pallas kernels for 15% -> 14%
where the time goes in v5:
time: 86.2 us; the launch traced here: 86 us
  blocking collectives  30.2 us (35%)
  Pallas kernels  23 us (27%)
  other arithmetic  19 us (22%)
  local copies, waits for them, and re-layouts  4.76 us (6%)
  matrix products  4.67 us (5%)
  starting transfers between devices  4.1 us (5%)
    all_to_all x1, blocking collectives, on_device(): lax.all_to_all(spectra, ('tm', 'stn'), split_axis=0, concat_axis=0, tiled...  30.2 us
    pallas_call x2, Pallas kernels, band_spectra(): pl.pallas_call(kernel, out_shape=jax.ShapeDtypeStruct((2, rows, band), jn...  23 us
    another operation x1, other arithmetic, band_tables(): return jnp.stack([hi, t - hi]).astype(jnp.bfloat16)  7.76 us
    dot_general x1, matrix products, on_device(): jnp.einsum('ki,kj->ij', both, stacked, preferred_element_type=jnp.float32)  4.67 us
    another operation x2, other arithmetic  4.59 us
    ppermute x1, starting transfers between devices, passed_along(): return lax.ppermute(x, axis, pairs)  4.1 us
    convert_element_type x1, other arithmetic, on_device(): spectra = jnp.stack([spec_re, spec_im], axis=2).astype(jnp.bfloat16)  2.21 us
  transfers between devices with their start and end apart: 1, of which 0 were waited for; matrix products, arithmetic and copies ran while one was open for 0% of the time, Pallas kernels for 14%

profile of v5, /device:TPU:1, one launch (start us, length us, event | category | flops | bytes accessed | tf_op | source)
XLA Modules:
  0.0 86.0 jit_solution(6538716430098782021)
XLA Ops:
  0.0 1.0 %fusion.17 = (f32[2,128,256]{2,1,0:T(8,128)S(1)}, f32[2,128,256]{2,1,0:T(8,128)S(1)}) fusion(s32[2,256]{1,0:T(2,128)S(1)} %get-tuple-element.29), kind=kLoop, calls=%fused_computation.38 | loop fusion | flops 983040 | bytes 526336 | tf_op jit(solution)/shard_map/cos | solution.py:53
  1.1 0.3 negate_select_fusion.4
  1.4 1.2 %multiply_add_fusion = f32[2,128,32,256]{3,2,1,0:T(8,128)S(1)} fusion(f32[2,32,256]{2,1,0:T(8,128)S(1)} %get-tuple-element.26, f32[2,128,256]{2,1,0:T(8,128)S(1)} %get-tuple-element.28, f32[2,32,256]{2,1,0:T(8,128)S(1)} %get-tuple-element.25, f32[2,128,256]{2,1,0:T(8,128)S(1)} %get-tuple-element.27), kind=kLoop, calls=%fused_computation.4 | loop fusion | flops 6291456 | bytes 9043968 | tf_op jit(solution)/shard_map/add | solution.py:57
  2.6 4.5 %reduce-precision_convert_fusion = (bf16[1,2,4096,256]{3,2,1,0:T(8,128)(2,1)}, bf16[1,2,4096,256]{3,2,1,0:T(8,128)(2,1)}) fusion(f32[1,2,4096,256]{3,2,1,0:T(8,128)S(1)} %bitcast.55), kind=kLoop, calls=%fused_computation.1 | loop fusion | flops 8388608 | bytes 16777216 | tf_op jit(solution)/shard_map/convert.2
  7.1 0.0 copy-start
  7.1 0.0 copy-start.1
  7.1 7.8 %pad_maximum_fusion.table_hbm = bf16[2,2,4096,256]{3,2,1,0:T(8,128)(2,1)} fusion(bf16[1,2,4096,256]{3,2,1,0:T(8,128)(2,1)} %get-tuple-element.18, bf16[1,2,4096,256]{3,2,1,0:T(8,128)(2,1)} %get-tuple-element.17), kind=kLoop, calls=%fused_computation.3 | loop fusion | flops 4194304 | bytes 16777216 | tf_op jit(solution)/shard_map/stack | solution.py:60
  14.9 0.0 copy-done
  14.9 0.0 copy-done.1
  14.9 11.0 %shard_map.38 = f32[2,224,256]{2,1,0:T(8,128)S(1)} custom-call(bf16[32,65536]{1,0:T(8,128)(2,1)S(1)} %copy-done, f32[8,8192]{1,0:T(8,128)S(1)} %copy-done.1, bf16[2,2,4096,256]{3,2,1,0:T(8,128)(2,1)} %pad_maximum_fusion.table_hbm), custom_call_target="tpu_custom_call" | custom-call | tf_op jit(solution)/shard_map/pallas_call | solution.py:145
  25.9 0.0 copy-start.2
  25.9 4.1 %collective-permute-start = (f32[2,224,256]{2,1,0:T(8,128)S(1)}, f32[2,224,256]{2,1,0:T(8,128)S(1)}, u32[]{:S(2)}, u32[]{:S(2)}) collective-permute-start(f32[2,224,256]{2,1,0:T(8,128)S(1)} %shard_map.38), channel_id=1, source_target_pairs={{0,32},{32,64},{64,96},{96,128},{128,160},{160,192},{192,224},{1,3... | collective-permute-start | bytes 1376264 | tf_op jit(solution)/shard_map/ppermute | solution.py:20
  30.1 12.0 %shard_map.37 = f32[2,256,256]{2,1,0:T(8,128)S(1)} custom-call(bf16[32,65536]{1,0:T(8,128)(2,1)S(1)} %copy-done, f32[8,8192]{1,0:T(8,128)S(1)} %copy-done.1, bf16[2,2,4096,256]{3,2,1,0:T(8,128)(2,1)} %pad_maximum_fusion.table_hbm), custom_call_target="tpu_custom_call" | custom-call | tf_op jit(solution)/shard_map/pallas_call | solution.py:145
  42.0 0.0 copy-done.2
  42.1 0.1 copy.20
  42.2 0.1 copy.21
  42.3 0.1 copy.23
  42.4 0.0 collective-permute-done
  42.4 0.1 fusion.6
  42.5 0.1 fusion.11
  42.7 0.2 copy.24
  42.8 0.2 convert_element_type.40
  43.1 0.5 broadcast.255
  43.6 2.2 %reduce.3 = bf16[256,512]{1,0:T(8,128)(2,1)S(1)} reduce(bf16[256,1,512]{2,1,0:T(2,128)(2,1)S(1)} %convert_element_type.40, bf16[]{:T(256)} %broadcast.255), dimensions={1}, to_apply=%convert_element_type.40.reduce_sub_computation | reduce | bytes 524290 | tf_op jit(solution)/shard_map/convert_element_type | solution.py:192
  45.8 0.1 reshape.352
  45.9 30.2 %all_to_all.6 = bf16[256,2,256]{2,1,0:T(2,128)(2,1)S(1)} all-to-all(bf16[256,2,256]{2,1,0:T(2,128)(2,1)S(1)} %reshape.352), channel_id=1, replica_groups=mesh['tm'=8,'stn'=32] {'tm','stn'}, dimensions={0} | all-to-all | bytes 524288 | tf_op jit(solution)/shard_map/all_to_all | solution.py:194
  76.1 0.2 reshape.353
  76.4 1.6 %reduce.2 = bf16[256,512]{1,0:T(8,128)(2,1)S(1)} reduce(bf16[256,1,512]{2,1,0:T(2,128)(2,1)S(1)} %reshape.353, bf16[]{:T(256)} %constant.84), dimensions={1}, to_apply=%all_to_all.4.reduce_sub_computation | reduce | bytes 524290 | tf_op jit(solution)/shard_map/all_to_all | solution.py:194
  77.9 0.6 reshape.349
  78.5 0.1 fusion.29
  78.7 0.3 copy.26
  79.0 0.1 copy.28
  79.1 0.5 neg.28
  79.6 0.1 copy.27
  79.7 0.5 squeeze.14
  80.2 1.1 %reshape_reshape.3 = bf16[128,1024]{1,0:T(8,128)(2,1)S(1)} reshape(bf16[2,8,8,32,32]{4,3,2,1,0:T(8,128)(2,1)S(1)} %copy.26) | data formatting | bytes 524288 | tf_op jit(solution)/shard_map/reshape;reshape | solution.py:198
  81.3 4.7 %convolution_multiply_fusion = f32[2048,1024]{1,0:T(8,128)} fusion(bf16[128,1024]{1,0:T(8,128)(2,1)S(1)} %reshape_reshape.3, bf16[64,1024]{1,0:T(8,128)(2,1)S(1)} %neg.28, bf16[64,1024]{1,0:T(8,128)(2,1)S(1)} %squeeze.14), kind=kOutput, calls=%fused_computation.5 | convolution fusion | flops 540540928 | bytes 8912896 | tf_op jit(solution)/shard_map/ki,kj->ij/dot_general | solution.py:200
  (6 shorter events, 0.1 us)
Async XLA Ops:
  7.1 7.8 %copy-start = (bf16[32,65536]{1,0:T(8,128)(2,1)S(1)}, bf16[32,65536]{1,0:T(8,128)(2,1)}, u32[]{:S(2)}) copy-start(bf16[32,65536]{1,0:T(8,128)(2,1)} %x_ref.3) | copy-start | bytes 12582916
  7.1 7.8 %copy-start.1 = (f32[8,8192]{1,0:T(8,128)S(1)}, f32[8,8192]{1,0:T(8,128)}, u32[]{:S(2)}) copy-start(f32[8,8192]{1,0:T(8,128)} %constant.83.clone.w_ref) | copy-start | bytes 786436
  25.9 16.1 %copy-start.2 = (f32[2,32,256]{2,1,0:T(8,128)S(1)}, f32[2,32,256]{2,1,0:T(8,128)}, u32[]{:S(2)}) copy-start(f32[2,32,256]{2,1,0:T(8,128)} %param.6) | copy-start | bytes 196612
  25.9 16.4 %collective-permute-start = (f32[2,224,256]{2,1,0:T(8,128)S(1)}, f32[2,224,256]{2,1,0:T(8,128)S(1)}, u32[]{:S(2)}, u32[]{:S(2)}) collective-permute-start(f32[2,224,256]{2,1,0:T(8,128)S(1)} %shard_map.38), channel_id=1, source_target_pairs={{0,32},{32,64},{64,96},{96,128},{128,160},{160,192},{192,224},{1,3... | collective-permute-start | bytes 1376264 | tf_op jit(solution)/shard_map/ppermute | solution.py:20

commit v6 on v5

--- a/solution.py
+++ b/solution.py
@@ -55,12 +55,10 @@
     b1 = jnp.where(imag_col, qi, qr)
     b2 = jnp.where(imag_col, qr, -qi)
     t = pr[:, :, None, :] * b1[:, None, :, :] + pi[:, :, None, :] * b2[:, None, :, :]
-    t = t.reshape(2, n_a * n_b, band)
-    hi = lax.reduce_precision(t, exponent_bits=8, mantissa_bits=7)
-    return jnp.stack([hi, t - hi]).astype(jnp.bfloat16)
-
-
-def taps_dft_kernel(x_ref, w_ref, table_hbm, out_ref, lhs_ref, th_ref, tl_ref, sem, *, first_slot, n_slots):
+    return t.reshape(2, n_a * n_b, band)
+
+
+def taps_dft_kernel(x_ref, w_ref, table_hbm, out_ref, lhs_ref, table_ref, sem, *, first_slot, n_slots):
     step = pl.program_id(0)
     steps = pl.num_programs(0)
     block = x_ref.shape[0]
@@ -70,13 +68,11 @@
     frames = x_ref.shape[1] // frame_len
     history = TAPS - 1
     lanes = 128
-    copy_hi = pltpu.make_async_copy(table_hbm.at[0], th_ref, sem.at[0])
-    copy_lo = pltpu.make_async_copy(table_hbm.at[1], tl_ref, sem.at[1])
+    copy_table = pltpu.make_async_copy(table_hbm, table_ref, sem.at[0])
 
     @pl.when(step == 0)
     def _():
-        copy_hi.start()
-        copy_lo.start()
+        copy_table.start()
 
     row0 = pl.multiple_of(step * block, block)
 
@@ -111,8 +107,7 @@
 
     @pl.when(step == steps - 1)
     def _():
-        copy_hi.wait()
-        copy_lo.wait()
+        copy_table.wait()
         depth = 512
         f32 = jnp.float32
         for q in range(2):
@@ -123,8 +118,9 @@
                 cols = pl.ds(k0, depth)
                 rows = lhs_ref.shape[2]
                 both = lhs_ref[q, :, :, cols].reshape(2 * rows, depth)
-                t_hi = th_ref[q, cols, :]
-                t_lo = tl_ref[q, cols, :]
+                table = table_ref[q, cols, :]
+                t_hi = table.astype(jnp.bfloat16)
+                t_lo = (table - t_hi.astype(f32)).astype(jnp.bfloat16)
                 acc = jnp.dot(both, t_hi, preferred_element_type=f32)
                 acc = acc[:rows] + acc[rows:]
                 acc = acc + jnp.dot(both[:rows], t_lo, preferred_element_type=f32)
@@ -138,7 +134,7 @@
     in_dev, length = voltages.shape
     frame_len = window.shape[1]
     half = frame_len // 2
-    band = table.shape[3]
+    band = table.shape[2]
     block = 16
     rows = n_slots * in_dev
     kernel = functools.partial(taps_dft_kernel, first_slot=first_slot, n_slots=n_slots)
@@ -154,9 +150,8 @@
         out_specs=pl.BlockSpec((2, rows, band), lambda g: (0, 0, 0)),
         scratch_shapes=[
             pltpu.VMEM((2, 2, rows, half), jnp.bfloat16),
-            pltpu.VMEM((2, half, band), jnp.bfloat16),
-            pltpu.VMEM((2, half, band), jnp.bfloat16),
-            pltpu.SemaphoreType.DMA((2,)),
+            pltpu.VMEM((2, half, band), jnp.float32),
+            pltpu.SemaphoreType.DMA((1,)),
         ],
         compiler_params=pltpu.CompilerParams(vmem_limit_bytes=48 * 1024 * 1024),
     )(voltages, window, table)

time: 86.2 us -> 77.5 us (0.90)
  other arithmetic: 19 us -> 10.1 us
    another operation x3 -> x1, other arithmetic: 12.4 us -> 0.07 us  [the longest x1 7.76 us: band_tables(): return jnp.stack([hi, t - hi]).astype(jnp.bfloat16)]
    add x1, other arithmetic: 1.23 us -> 4.58 us  [band_tables(): pr[:, :, None, :] * b1[:, None, :, :]]
  transfers between devices with their start and end apart: 1 -> 1, of which waited for: 0 -> 0; matrix products, arithmetic and copies ran while one was open for 0% -> 0% of each run, Pallas kernels for 14% -> 16%
where the time goes in v6:
time: 77.5 us; the launch traced here: 77.3 us
  blocking collectives  30.2 us (39%)
  Pallas kernels  23.3 us (30%)
  other arithmetic  10.1 us (13%)
  local copies, waits for them, and re-layouts  4.76 us (6%)
  matrix products  4.67 us (6%)
  starting transfers between devices  4.1 us (5%)
    all_to_all x1, blocking collectives, on_device(): lax.all_to_all(spectra, ('tm', 'stn'), split_axis=0, concat_axis=0, tiled...  30.2 us
    pallas_call x2, Pallas kernels, band_spectra(): pl.pallas_call(kernel, out_shape=jax.ShapeDtypeStruct((2, rows, band), jn...  23.3 us
    dot_general x1, matrix products, on_device(): jnp.einsum('ki,kj->ij', both, stacked, preferred_element_type=jnp.float32)  4.67 us
    add x1, other arithmetic, band_tables(): pr[:, :, None, :] * b1[:, None, :, :]  4.58 us
    ppermute x1, starting transfers between devices, passed_along(): return lax.ppermute(x, axis, pairs)  4.1 us
    convert_element_type x1, other arithmetic, on_device(): spectra = jnp.stack([spec_re, spec_im], axis=2).astype(jnp.bfloat16)  2.21 us
    all_to_all x1, other arithmetic, on_device(): lax.all_to_all(spectra, ('tm', 'stn'), split_axis=0, concat_axis=0, tiled...  1.56 us
  transfers between devices with their start and end apart: 1, of which 0 were waited for; matrix products, arithmetic and copies ran while one was open for 0% of the time, Pallas kernels for 16%

profile of v6, /device:TPU:1, one launch (start us, length us, event | category | flops | bytes accessed | tf_op | source)
XLA Modules:
  0.0 77.3 jit_solution(3021346303249139527)
XLA Ops:
  0.0 0.0 copy-start.1
  0.0 0.0 copy-start
  0.0 1.0 %fusion.16 = (f32[2,128,256]{2,1,0:T(8,128)S(1)}, f32[2,128,256]{2,1,0:T(8,128)S(1)}) fusion(s32[2,256]{1,0:T(2,128)S(1)} %get-tuple-element.27), kind=kLoop, calls=%fused_computation.34 | loop fusion | flops 983040 | bytes 526336 | tf_op jit(solution)/shard_map/cos | solution.py:53
  1.1 0.3 negate_select_fusion.4
  1.4 4.6 %multiply_add_fusion = f32[2,128,32,256]{3,2,1,0:T(8,128)} fusion(f32[2,32,256]{2,1,0:T(8,128)S(1)} %get-tuple-element.24, f32[2,128,256]{2,1,0:T(8,128)S(1)} %get-tuple-element.26, f32[2,32,256]{2,1,0:T(8,128)S(1)} %get-tuple-element.23, f32[2,128,256]{2,1,0:T(8,128)S(1)} %get-tuple-element.25), kind=kLoop, calls=%fused_computation | loop fusion | flops 6291456 | bytes 9043968 | tf_op jit(solution)/shard_map/add | solution.py:57
  6.0 0.0 copy-done.1
  6.0 0.0 copy-done
  6.0 11.2 %shard_map.38 = f32[2,224,256]{2,1,0:T(8,128)S(1)} custom-call(bf16[32,65536]{1,0:T(8,128)(2,1)S(1)} %copy-done, f32[8,8192]{1,0:T(8,128)S(1)} %copy-done.1, f32[2,4096,256]{2,1,0:T(8,128)} %bitcast.55), custom_call_target="tpu_custom_call" | custom-call | tf_op jit(solution)/shard_map/pallas_call | solution.py:141
  17.2 0.0 copy-start.2
  17.2 4.1 %collective-permute-start = (f32[2,224,256]{2,1,0:T(8,128)S(1)}, f32[2,224,256]{2,1,0:T(8,128)S(1)}, u32[]{:S(2)}, u32[]{:S(2)}) collective-permute-start(f32[2,224,256]{2,1,0:T(8,128)S(1)} %shard_map.38), channel_id=1, source_target_pairs={{0,32},{32,64},{64,96},{96,128},{128,160},{160,192},{192,224},{1,3... | collective-permute-start | bytes 1376264 | tf_op jit(solution)/shard_map/ppermute | solution.py:20
  21.3 12.1 %shard_map.37 = f32[2,256,256]{2,1,0:T(8,128)S(1)} custom-call(bf16[32,65536]{1,0:T(8,128)(2,1)S(1)} %copy-done, f32[8,8192]{1,0:T(8,128)S(1)} %copy-done.1, f32[2,4096,256]{2,1,0:T(8,128)} %bitcast.56), custom_call_target="tpu_custom_call" | custom-call | tf_op jit(solution)/shard_map/pallas_call | solution.py:141
  33.4 0.0 copy-done.2
  33.4 0.1 copy.20
  33.5 0.1 copy.21
  33.6 0.1 copy.23
  33.7 0.0 collective-permute-done
  33.7 0.1 fusion.5
  33.9 0.1 fusion.10
  34.0 0.2 copy.24
  34.2 0.2 convert_element_type.39
  34.4 0.5 broadcast.255
  34.9 2.2 %reduce.3 = bf16[256,512]{1,0:T(8,128)(2,1)S(1)} reduce(bf16[256,1,512]{2,1,0:T(2,128)(2,1)S(1)} %convert_element_type.39, bf16[]{:T(256)} %broadcast.255), dimensions={1}, to_apply=%convert_element_type.39.reduce_sub_computation | reduce | bytes 524290 | tf_op jit(solution)/shard_map/convert_element_type | solution.py:187
  37.1 0.1 reshape.293
  37.2 30.2 %all_to_all.6 = bf16[256,2,256]{2,1,0:T(2,128)(2,1)S(1)} all-to-all(bf16[256,2,256]{2,1,0:T(2,128)(2,1)S(1)} %reshape.293), channel_id=1, replica_groups=mesh['tm'=8,'stn'=32] {'tm','stn'}, dimensions={0} | all-to-all | bytes 524288 | tf_op jit(solution)/shard_map/all_to_all | solution.py:189
  67.4 0.2 reshape.294
  67.7 1.6 %reduce.2 = bf16[256,512]{1,0:T(8,128)(2,1)S(1)} reduce(bf16[256,1,512]{2,1,0:T(2,128)(2,1)S(1)} %reshape.294, bf16[]{:T(256)} %constant.84), dimensions={1}, to_apply=%all_to_all.4.reduce_sub_computation | reduce | bytes 524290 | tf_op jit(solution)/shard_map/all_to_all | solution.py:189
  69.2 0.6 reshape.290
  69.8 0.1 fusion.28
  70.0 0.3 copy.26
  70.3 0.1 copy.28
  70.4 0.5 neg.28
  70.9 0.1 copy.27
  71.0 0.5 squeeze.14
  71.5 1.1 %reshape_reshape.3 = bf16[128,1024]{1,0:T(8,128)(2,1)S(1)} reshape(bf16[2,8,8,32,32]{4,3,2,1,0:T(8,128)(2,1)S(1)} %copy.26) | data formatting | bytes 524288 | tf_op jit(solution)/shard_map/reshape;reshape | solution.py:193
  72.6 4.7 %convolution_multiply_fusion = f32[2048,1024]{1,0:T(8,128)} fusion(bf16[128,1024]{1,0:T(8,128)(2,1)S(1)} %reshape_reshape.3, bf16[64,1024]{1,0:T(8,128)(2,1)S(1)} %neg.28, bf16[64,1024]{1,0:T(8,128)(2,1)S(1)} %squeeze.14), kind=kOutput, calls=%fused_computation.1 | convolution fusion | flops 540540928 | bytes 8912896 | tf_op jit(solution)/shard_map/ki,kj->ij/dot_general | solution.py:195
  (6 shorter events, 0.1 us)
Async XLA Ops:
  0.0 6.0 %copy-start.1 = (f32[8,8192]{1,0:T(8,128)S(1)}, f32[8,8192]{1,0:T(8,128)}, u32[]{:S(2)}) copy-start(f32[8,8192]{1,0:T(8,128)} %constant.83.clone.w_ref) | copy-start | bytes 786436
  0.0 6.0 %copy-start = (bf16[32,65536]{1,0:T(8,128)(2,1)S(1)}, bf16[32,65536]{1,0:T(8,128)(2,1)}, u32[]{:S(2)}) copy-start(bf16[32,65536]{1,0:T(8,128)(2,1)} %x_ref.3) | copy-start | bytes 12582916
  17.2 16.2 %copy-start.2 = (f32[2,32,256]{2,1,0:T(8,128)S(1)}, f32[2,32,256]{2,1,0:T(8,128)}, u32[]{:S(2)}) copy-start(f32[2,32,256]{2,1,0:T(8,128)} %param.6) | copy-start | bytes 196612
  17.2 16.5 %collective-permute-start = (f32[2,224,256]{2,1,0:T(8,128)S(1)}, f32[2,224,256]{2,1,0:T(8,128)S(1)}, u32[]{:S(2)}, u32[]{:S(2)}) collective-permute-start(f32[2,224,256]{2,1,0:T(8,128)S(1)} %shard_map.38), channel_id=1, source_target_pairs={{0,32},{32,64},{64,96},{96,128},{128,160},{160,192},{192,224},{1,3... | collective-permute-start | bytes 1376264 | tf_op jit(solution)/shard_map/ppermute | solution.py:20

commit v7 on v6

--- a/solution.py
+++ b/solution.py
@@ -59,29 +59,26 @@
 
 
 def taps_dft_kernel(x_ref, w_ref, table_hbm, out_ref, lhs_ref, table_ref, sem, *, first_slot, n_slots):
-    step = pl.program_id(0)
-    steps = pl.num_programs(0)
-    block = x_ref.shape[0]
-    inputs = block * steps
+    inputs = x_ref.shape[0]
+    sub = 16
     frame_len = w_ref.shape[1]
     half = frame_len // 2
     frames = x_ref.shape[1] // frame_len
     history = TAPS - 1
     lanes = 128
+    depth = 512
+    spans = half // depth
+    rows = lhs_ref.shape[2]
+    f32 = jnp.float32
     copy_table = pltpu.make_async_copy(table_hbm, table_ref, sem.at[0])
-
-    @pl.when(step == 0)
-    def _():
-        copy_table.start()
-
-    row0 = pl.multiple_of(step * block, block)
-
-    def chunk(j, carry):
-        base = pl.multiple_of(j * lanes, lanes)
+    copy_table.start()
+
+    def taps(base, row0):
         xs = []
         ws = []
+        inputs_at = pl.ds(row0, sub)
         for offset in (0, half):
-            xs.append([x_ref[:, pl.ds(f * frame_len + offset + base, lanes)].astype(jnp.float32) for f in range(frames)])
+            xs.append([x_ref[inputs_at, pl.ds(f * frame_len + offset + base, lanes)].astype(f32) for f in range(frames)])
             ws.append([w_ref[pl.ds(p, 1), pl.ds(offset + base, lanes)] for p in range(TAPS)])
         for slot in range(n_slots):
             s = first_slot + slot
@@ -95,39 +92,45 @@
                         acc = term if acc is None else acc + term
                 accs.append(acc)
             folded = (accs[0] + accs[1], accs[0] - accs[1])
-            rows = pl.ds(pl.multiple_of(slot * inputs + row0, block), block)
+            at = pl.ds(slot * inputs + row0, sub)
             for q in range(2):
                 hi = folded[q].astype(jnp.bfloat16)
-                lo = (folded[q] - hi.astype(jnp.float32)).astype(jnp.bfloat16)
-                lhs_ref[q, 0, rows, pl.ds(base, lanes)] = hi
-                lhs_ref[q, 1, rows, pl.ds(base, lanes)] = lo
+                lo = (folded[q] - hi.astype(f32)).astype(jnp.bfloat16)
+                lhs_ref[q, 0, at, pl.ds(base, lanes)] = hi
+                lhs_ref[q, 1, at, pl.ds(base, lanes)] = lo
+
+    def taps_span(kk):
+        for c in range(depth // lanes):
+            base = pl.multiple_of(kk * depth + c * lanes, lanes)
+            for row0 in range(0, inputs, sub):
+                taps(base, row0)
+
+    def product(kk):
+        k0 = pl.multiple_of(kk * depth, depth)
+        cols = pl.ds(k0, depth)
+        for q in range(2):
+            both = lhs_ref[q, :, :, cols].reshape(2 * rows, depth)
+            table = table_ref[q, cols, :]
+            t_hi = table.astype(jnp.bfloat16)
+            t_lo = (table - t_hi.astype(f32)).astype(jnp.bfloat16)
+            acc = jnp.dot(both, t_hi, preferred_element_type=f32)
+            acc = acc[:rows] + acc[rows:]
+            acc = acc + jnp.dot(both[:rows], t_lo, preferred_element_type=f32)
+            out_ref[q] += acc
+
+    out_ref[...] = jnp.zeros(out_ref.shape, f32)
+    taps_span(0)
+    taps_span(1)
+    copy_table.wait()
+    product(0)
+
+    def span(kk, carry):
+        taps_span(kk)
+        product(kk - 1)
         return carry
 
-    lax.fori_loop(0, half // lanes, chunk, 0)
-
-    @pl.when(step == steps - 1)
-    def _():
-        copy_table.wait()
-        depth = 512
-        f32 = jnp.float32
-        for q in range(2):
-            out_ref[q] = jnp.zeros(out_ref.shape[1:], f32)
-
-            def kstep(kk, carry):
-                k0 = pl.multiple_of(kk * depth, depth)
-                cols = pl.ds(k0, depth)
-                rows = lhs_ref.shape[2]
-                both = lhs_ref[q, :, :, cols].reshape(2 * rows, depth)
-                table = table_ref[q, cols, :]
-                t_hi = table.astype(jnp.bfloat16)
-                t_lo = (table - t_hi.astype(f32)).astype(jnp.bfloat16)
-                acc = jnp.dot(both, t_hi, preferred_element_type=f32)
-                acc = acc[:rows] + acc[rows:]
-                acc = acc + jnp.dot(both[:rows], t_lo, preferred_element_type=f32)
-                out_ref[q] += acc
-                return carry
-
-            lax.fori_loop(0, half // depth, kstep, 0)
+    lax.fori_loop(2, spans, span, 0)
+    product(spans - 1)
 
 
 def band_spectra(voltages, window, table, frames, first_slot, n_slots):
@@ -135,15 +138,14 @@
     frame_len = window.shape[1]
     half = frame_len // 2
     band = table.shape[2]
-    block = 16
     rows = n_slots * in_dev
     kernel = functools.partial(taps_dft_kernel, first_slot=first_slot, n_slots=n_slots)
     return pl.pallas_call(
         kernel,
         out_shape=jax.ShapeDtypeStruct((2, rows, band), jnp.float32),
-        grid=(in_dev // block,),
+        grid=(1,),
         in_specs=[
-            pl.BlockSpec((block, length), lambda g: (g, 0)),
+            pl.BlockSpec((in_dev, length), lambda g: (0, 0)),
             pl.BlockSpec((TAPS, frame_len), lambda g: (0, 0)),
             pl.BlockSpec(memory_space=pl.ANY),
         ],
@@ -153,7 +155,7 @@
             pltpu.VMEM((2, half, band), jnp.float32),
             pltpu.SemaphoreType.DMA((1,)),
         ],
-        compiler_params=pltpu.CompilerParams(vmem_limit_bytes=48 * 1024 * 1024),
+        compiler_params=pltpu.CompilerParams(vmem_limit_bytes=56 * 1024 * 1024),
     )(voltages, window, table)
 
 

time: 77.5 us -> 85.3 us (1.10)
  Pallas kernels: 23.3 us -> 28.1 us
  other arithmetic: 10.1 us -> 11.8 us
  local copies, waits for them, and re-layouts: 4.76 us -> 5.79 us
    pallas_call x2, Pallas kernels: 23.3 us -> 28.1 us  [band_spectra(): pl.pallas_call(kernel, out_shape=jax.ShapeDtypeStruct((2, rows, band), jn...]
    scatter-add x1, other arithmetic: 0.13 us -> 1.87 us  [on_device(): raw = raw.at[:, :history * in_dev, :].add(given)]
    transpose x1, local copies, waits for them, and re-layouts: 0.04 us -> 1.08 us  [on_device(): raw = jnp.transpose(raw.reshape(2, 2, half_band, row), (1, 2, 0, 3))]
  transfers between devices with their start and end apart: 1 -> 1, of which waited for: 0 -> 0; matrix products, arithmetic and copies ran while one was open for 0% -> 0% of each run, Pallas kernels for 16% -> 17%
where the time goes in v7:
time: 85.3 us; the launch traced here: 85 us
  blocking collectives  30.2 us (35%)
  Pallas kernels  28.1 us (33%)
  other arithmetic  11.8 us (14%)
  local copies, waits for them, and re-layouts  5.79 us (7%)
  matrix products  4.68 us (5%)
  starting transfers between devices  4.11 us (5%)
    all_to_all x1, blocking collectives, on_device(): lax.all_to_all(spectra, ('tm', 'stn'), split_axis=0, concat_axis=0, tiled...  30.2 us
    pallas_call x2, Pallas kernels, band_spectra(): pl.pallas_call(kernel, out_shape=jax.ShapeDtypeStruct((2, rows, band), jn...  28.1 us
    dot_general x1, matrix products, on_device(): jnp.einsum('ki,kj->ij', both, stacked, preferred_element_type=jnp.float32)  4.68 us
    add x1, other arithmetic, band_tables(): pr[:, :, None, :] * b1[:, None, :, :]  4.58 us
    ppermute x1, starting transfers between devices, passed_along(): return lax.ppermute(x, axis, pairs)  4.11 us
    convert_element_type x1, other arithmetic, on_device(): spectra = jnp.stack([spec_re, spec_im], axis=2).astype(jnp.bfloat16)  2.21 us
    scatter-add x1, other arithmetic, on_device(): raw = raw.at[:, :history * in_dev, :].add(given)  1.87 us
  transfers between devices with their start and end apart: 1, of which 0 were waited for; matrix products, arithmetic and copies ran while one was open for 0% of the time, Pallas kernels for 17%

profile of v7, /device:TPU:1, one launch (start us, length us, event | category | flops | bytes accessed | tf_op | source)
XLA Modules:
  0.0 85.0 jit_solution(8935224803271030797)
XLA Ops:
  0.0 1.0 %fusion.16 = (f32[2,128,256]{2,1,0:T(8,128)S(1)}, f32[2,128,256]{2,1,0:T(8,128)S(1)}) fusion(s32[2,256]{1,0:T(2,128)S(1)} %get-tuple-element.27), kind=kLoop, calls=%fused_computation.34 | loop fusion | flops 983040 | bytes 526336 | tf_op jit(solution)/shard_map/cos | solution.py:53
  1.1 0.3 negate_select_fusion.4
  1.4 4.6 %multiply_add_fusion = f32[2,128,32,256]{3,2,1,0:T(8,128)} fusion(f32[2,32,256]{2,1,0:T(8,128)S(1)} %get-tuple-element.24, f32[2,128,256]{2,1,0:T(8,128)S(1)} %get-tuple-element.26, f32[2,32,256]{2,1,0:T(8,128)S(1)} %get-tuple-element.23, f32[2,128,256]{2,1,0:T(8,128)S(1)} %get-tuple-element.25), kind=kLoop, calls=%fused_computation | loop fusion | flops 6291456 | bytes 9043968 | tf_op jit(solution)/shard_map/add | solution.py:57
  5.9 13.6 %shard_map.38 = f32[2,224,256]{2,1,0:T(8,128)} custom-call(bf16[32,65536]{1,0:T(8,128)(2,1)} %x_ref.3, f32[8,8192]{1,0:T(8,128)} %constant.83.clone.w_ref, f32[2,4096,256]{2,1,0:T(8,128)} %bitcast.55), custom_call_target="tpu_custom_call" | custom-call | tf_op jit(solution)/shard_map/pallas_call | solution.py:143
  19.6 0.0 copy-start
  19.6 4.1 %collective-permute-start = (f32[2,224,256]{2,1,0:T(8,128)}, f32[2,224,256]{2,1,0:T(8,128)S(1)}, u32[]{:S(2)}, u32[]{:S(2)}) collective-permute-start(f32[2,224,256]{2,1,0:T(8,128)} %shard_map.38), channel_id=1, source_target_pairs={{0,32},{32,64},{64,96},{96,128},{128,160},{160,192},{192,224},{1,3... | collective-permute-start | bytes 1376264 | tf_op jit(solution)/shard_map/ppermute | solution.py:20
  23.7 14.5 %shard_map.37 = f32[2,256,256]{2,1,0:T(8,128)} custom-call(bf16[32,65536]{1,0:T(8,128)(2,1)} %x_ref.3, f32[8,8192]{1,0:T(8,128)} %constant.83.clone.w_ref, f32[2,4096,256]{2,1,0:T(8,128)} %bitcast.56), custom_call_target="tpu_custom_call" | custom-call | tf_op jit(solution)/shard_map/pallas_call | solution.py:143
  38.2 0.0 copy-done
  38.2 0.1 copy.20
  38.4 0.1 copy.21
  38.5 0.1 copy.23
  38.5 0.0 collective-permute-done
  38.5 1.9 %fusion.5 = f32[2,256,256]{2,1,0:T(8,128)} fusion(f32[2,256,256]{2,1,0:T(8,128)} %shard_map.37, f32[2,224,256]{2,1,0:T(8,128)S(1)} %collective-permute-done), kind=kLoop, calls=%fused_computation.10 | loop fusion | flops 114688 | bytes 1376256 | tf_op jit(solution)/shard_map/scatter-add | solution.py:178
  40.4 1.1 %bitcast_bitcast_fusion = f32[2,128,2,256]{1,3,2,0:T(8,128)S(1)} fusion(f32[2,256,256]{2,1,0:T(8,128)} %fusion.5), kind=kLoop, calls=%fused_computation.2 | loop fusion | bytes 1048576 | tf_op jit(solution)/shard_map/transpose | solution.py:182
  41.5 0.1 fusion.10
  41.6 0.2 copy.24
  41.8 0.2 convert_element_type.39
  42.0 0.5 broadcast.255
  42.6 2.2 %reduce.3 = bf16[256,512]{1,0:T(8,128)(2,1)S(1)} reduce(bf16[256,1,512]{2,1,0:T(2,128)(2,1)S(1)} %convert_element_type.39, bf16[]{:T(256)} %broadcast.255), dimensions={1}, to_apply=%convert_element_type.39.reduce_sub_computation | reduce | bytes 524290 | tf_op jit(solution)/shard_map/convert_element_type | solution.py:189
  44.8 0.1 reshape.293
  44.8 30.2 %all_to_all.6 = bf16[256,2,256]{2,1,0:T(2,128)(2,1)S(1)} all-to-all(bf16[256,2,256]{2,1,0:T(2,128)(2,1)S(1)} %reshape.293), channel_id=1, replica_groups=mesh['tm'=8,'stn'=32] {'tm','stn'}, dimensions={0} | all-to-all | bytes 524288 | tf_op jit(solution)/shard_map/all_to_all | solution.py:191
  75.1 0.2 reshape.294
  75.3 1.6 %reduce.2 = bf16[256,512]{1,0:T(8,128)(2,1)S(1)} reduce(bf16[256,1,512]{2,1,0:T(2,128)(2,1)S(1)} %reshape.294, bf16[]{:T(256)} %constant.84), dimensions={1}, to_apply=%all_to_all.4.reduce_sub_computation | reduce | bytes 524290 | tf_op jit(solution)/shard_map/all_to_all | solution.py:191
  76.9 0.6 reshape.290
  77.5 0.1 fusion.28
  77.6 0.3 copy.26
  77.9 0.1 copy.28
  78.0 0.5 neg.28
  78.5 0.1 copy.27
  78.6 0.5 squeeze.14
  79.2 1.1 %reshape_reshape.3 = bf16[128,1024]{1,0:T(8,128)(2,1)S(1)} reshape(bf16[2,8,8,32,32]{4,3,2,1,0:T(8,128)(2,1)S(1)} %copy.26) | data formatting | bytes 524288 | tf_op jit(solution)/shard_map/reshape;reshape | solution.py:195
  80.3 4.7 %convolution_multiply_fusion = f32[2048,1024]{1,0:T(8,128)} fusion(bf16[128,1024]{1,0:T(8,128)(2,1)S(1)} %reshape_reshape.3, bf16[64,1024]{1,0:T(8,128)(2,1)S(1)} %neg.28, bf16[64,1024]{1,0:T(8,128)(2,1)S(1)} %squeeze.14), kind=kOutput, calls=%fused_computation.1 | convolution fusion | flops 540540928 | bytes 8912896 | tf_op jit(solution)/shard_map/ki,kj->ij/dot_general | solution.py:197
  (5 shorter events, 0.1 us)
Async XLA Ops:
  19.6 18.6 %copy-start = (f32[2,32,256]{2,1,0:T(8,128)S(1)}, f32[2,32,256]{2,1,0:T(8,128)}, u32[]{:S(2)}) copy-start(f32[2,32,256]{2,1,0:T(8,128)} %param.6) | copy-start | bytes 196612
  19.6 18.9 %collective-permute-start = (f32[2,224,256]{2,1,0:T(8,128)}, f32[2,224,256]{2,1,0:T(8,128)S(1)}, u32[]{:S(2)}, u32[]{:S(2)}) collective-permute-start(f32[2,224,256]{2,1,0:T(8,128)} %shard_map.38), channel_id=1, source_target_pairs={{0,32},{32,64},{64,96},{96,128},{128,160},{160,192},{192,224},{1,3... | collective-permute-start | bytes 1376264 | tf_op jit(solution)/shard_map/ppermute | solution.py:20

commit v8 on v6

--- a/solution.py
+++ b/solution.py
@@ -157,6 +157,28 @@
     )(voltages, window, table)
 
 
+def cross_kernel(lhs_ref, rhs_ref, out_ref, *, scale):
+    nt = (((1,), (1,)), ((), ()))
+    out = lax.dot_general(lhs_ref[...], rhs_ref[...], nt, preferred_element_type=jnp.float32)
+    out_ref[...] = out * scale
+
+
+def cross_power(both, stacked, scale):
+    rows, depth = both.shape
+    cols = stacked.shape[0]
+    block = 256
+    return pl.pallas_call(
+        functools.partial(cross_kernel, scale=scale),
+        out_shape=jax.ShapeDtypeStruct((rows, cols), jnp.float32),
+        grid=(rows // block,),
+        in_specs=[
+            pl.BlockSpec((block, depth), lambda g: (g, 0)),
+            pl.BlockSpec((cols, depth), lambda g: (0, 0)),
+        ],
+        out_specs=pl.BlockSpec((block, cols), lambda g: (g, 0)),
+    )(both, stacked)
+
+
 def on_device(voltages, gains):
     in_dev, length = voltages.shape
     band = gains.shape[2]
@@ -188,12 +210,11 @@
     spectra = spectra.reshape(n_time * n_station, 2 * row)
     spectra = lax.all_to_all(spectra, ("tm", "stn"), split_axis=0, concat_axis=0, tiled=True)
     spectra = spectra.reshape(n_time, n_station, 2, frames, in_dev)
-    stacked = jnp.transpose(spectra, (2, 0, 3, 1, 4)).reshape(2, n_time * frames, all_inputs)
-    flipped = jnp.concatenate([stacked[1], -stacked[0]], axis=0)
-    stacked = stacked.reshape(2 * n_time * frames, all_inputs)
-    both = jnp.concatenate([stacked, flipped], axis=1)
-    vis = jnp.einsum("ki,kj->ij", both, stacked, preferred_element_type=jnp.float32)
-    vis = vis * (1.0 / float(n_time * frames))
+    stacked = jnp.transpose(spectra, (1, 4, 2, 0, 3)).reshape(all_inputs, 2, n_time * frames)
+    flipped = jnp.concatenate([stacked[:, 1], -stacked[:, 0]], axis=1)
+    stacked = stacked.reshape(all_inputs, 2 * n_time * frames)
+    both = jnp.concatenate([stacked, flipped], axis=0)
+    vis = cross_power(both, stacked, 1.0 / float(n_time * frames))
     return vis.reshape(1, 2, all_inputs, all_inputs)
 
 

time: 77.5 us -> 81.3 us (1.049)
  Pallas kernels: 23.3 us -> 30.3 us
  matrix products: 4.67 us -> 0 us
    pallas_call x0 -> x1, Pallas kernels: none -> 6.99 us  [cross_power(): pl.pallas_call(functools.partial(cross_kernel, scale=scale), out_shape=ja...]
    dot_general x1 -> x0, matrix products: 4.67 us -> none  [on_device(): jnp.einsum('ki,kj->ij', both, stacked, preferred_element_type=jnp.float32)]
    reshape x0 -> x1, local copies, waits for them, and re-layouts: none -> 1.09 us  [on_device(): jnp.transpose(spectra, (1, 4, 2, 0, 3))]
    concatenate x0 -> x1, other arithmetic: none -> 0.94 us  [on_device(): both = jnp.concatenate([stacked, flipped], axis=0)]
  transfers between devices with their start and end apart: 1 -> 1, of which waited for: 0 -> 0; matrix products, arithmetic and copies ran while one was open for 0% -> 0% of each run, Pallas kernels for 16% -> 15%
where the time goes in v8:
time: 81.3 us; the launch traced here: 80.9 us
  Pallas kernels  30.3 us (37%)
  blocking collectives  30.2 us (37%)
  other arithmetic  10.9 us (13%)
  local copies, waits for them, and re-layouts  5.13 us (6%)
  starting transfers between devices  4.1 us (5%)
    all_to_all x1, blocking collectives, on_device(): lax.all_to_all(spectra, ('tm', 'stn'), split_axis=0, concat_axis=0, tiled...  30.2 us
    pallas_call x2, Pallas kernels, band_spectra(): pl.pallas_call(kernel, out_shape=jax.ShapeDtypeStruct((2, rows, band), jn...  23.3 us
    pallas_call x1, Pallas kernels, cross_power(): pl.pallas_call(functools.partial(cross_kernel, scale=scale), out_shape=ja...  6.99 us
    add x1, other arithmetic, band_tables(): pr[:, :, None, :] * b1[:, None, :, :]  4.58 us
    ppermute x1, starting transfers between devices, passed_along(): return lax.ppermute(x, axis, pairs)  4.1 us
    convert_element_type x1, other arithmetic, on_device(): spectra = jnp.stack([spec_re, spec_im], axis=2).astype(jnp.bfloat16)  2.21 us
  transfers between devices with their start and end apart: 1, of which 0 were waited for; matrix products, arithmetic and copies ran while one was open for 0% of the time, Pallas kernels for 15%

profile of v8, /device:TPU:1, one launch (start us, length us, event | category | flops | bytes accessed | tf_op | source)
XLA Modules:
  0.0 80.9 jit_solution(2644846231142200797)
XLA Ops:
  0.0 0.0 copy-start.1
  0.0 0.0 copy-start
  0.0 1.0 %fusion.11 = (f32[2,128,256]{2,1,0:T(8,128)S(1)}, f32[2,128,256]{2,1,0:T(8,128)S(1)}) fusion(s32[2,256]{1,0:T(2,128)S(1)} %get-tuple-element.27), kind=kLoop, calls=%fused_computation.29 | loop fusion | flops 983040 | bytes 526336 | tf_op jit(solution)/shard_map/cos | solution.py:53
  1.1 0.3 negate_select_fusion.4
  1.4 4.6 %multiply_add_fusion = f32[2,128,32,256]{3,2,1,0:T(8,128)} fusion(f32[2,32,256]{2,1,0:T(8,128)S(1)} %get-tuple-element.24, f32[2,128,256]{2,1,0:T(8,128)S(1)} %get-tuple-element.26, f32[2,32,256]{2,1,0:T(8,128)S(1)} %get-tuple-element.23, f32[2,128,256]{2,1,0:T(8,128)S(1)} %get-tuple-element.25), kind=kLoop, calls=%fused_computation | loop fusion | flops 6291456 | bytes 9043968 | tf_op jit(solution)/shard_map/add | solution.py:57
  6.0 0.0 copy-done.1
  6.0 0.0 copy-done
  6.0 11.2 %shard_map.38 = f32[2,224,256]{2,1,0:T(8,128)S(1)} custom-call(bf16[32,65536]{1,0:T(8,128)(2,1)S(1)} %copy-done, f32[8,8192]{1,0:T(8,128)S(1)} %copy-done.1, f32[2,4096,256]{2,1,0:T(8,128)} %bitcast.59), custom_call_target="tpu_custom_call" | custom-call | tf_op jit(solution)/shard_map/pallas_call | solution.py:141
  17.2 0.0 copy-start.3
  17.2 4.1 %collective-permute-start = (f32[2,224,256]{2,1,0:T(8,128)S(1)}, f32[2,224,256]{2,1,0:T(8,128)S(1)}, u32[]{:S(2)}, u32[]{:S(2)}) collective-permute-start(f32[2,224,256]{2,1,0:T(8,128)S(1)} %shard_map.38), channel_id=1, source_target_pairs={{0,32},{32,64},{64,96},{96,128},{128,160},{160,192},{192,224},{1,3... | collective-permute-start | bytes 1376264 | tf_op jit(solution)/shard_map/ppermute | solution.py:20
  21.3 12.1 %shard_map.37 = f32[2,256,256]{2,1,0:T(8,128)S(1)} custom-call(bf16[32,65536]{1,0:T(8,128)(2,1)S(1)} %copy-done, f32[8,8192]{1,0:T(8,128)S(1)} %copy-done.1, f32[2,4096,256]{2,1,0:T(8,128)} %bitcast.60), custom_call_target="tpu_custom_call" | custom-call | tf_op jit(solution)/shard_map/pallas_call | solution.py:141
  33.4 0.0 copy-done.3
  33.4 0.1 copy.27
  33.5 0.1 copy.28
  33.6 0.1 copy.30
  33.7 0.0 collective-permute-done
  33.7 0.1 fusion
  33.9 0.1 fusion.5
  34.0 0.2 copy.31
  34.2 0.2 convert_element_type.39
  34.4 0.5 broadcast.255
  34.9 2.2 %reduce.3 = bf16[256,512]{1,0:T(8,128)(2,1)S(1)} reduce(bf16[256,1,512]{2,1,0:T(2,128)(2,1)S(1)} %convert_element_type.39, bf16[]{:T(256)} %broadcast.255), dimensions={1}, to_apply=%convert_element_type.39.reduce_sub_computation | reduce | bytes 524290 | tf_op jit(solution)/shard_map/convert_element_type | solution.py:209
  37.1 0.1 reshape.292
  37.2 30.2 %all_to_all.6 = bf16[256,2,256]{2,1,0:T(2,128)(2,1)S(1)} all-to-all(bf16[256,2,256]{2,1,0:T(2,128)(2,1)S(1)} %reshape.292), channel_id=1, replica_groups=mesh['tm'=8,'stn'=32] {'tm','stn'}, dimensions={0} | all-to-all | bytes 524288 | tf_op jit(solution)/shard_map/all_to_all | solution.py:211
  67.4 0.2 reshape.293
  67.7 1.6 %reduce.2 = bf16[256,512]{1,0:T(8,128)(2,1)S(1)} reduce(bf16[256,1,512]{2,1,0:T(2,128)(2,1)S(1)} %reshape.293, bf16[]{:T(256)} %constant.82), dimensions={1}, to_apply=%all_to_all.4.reduce_sub_computation | reduce | bytes 524290 | tf_op jit(solution)/shard_map/all_to_all | solution.py:211
  69.2 0.6 reshape.288
  69.8 0.3 copy.33
  70.1 1.1 %reshape.289 = bf16[1024,2,64]{0,2,1:T(8,128)(2,1)S(1)} reshape(bf16[32,32,2,8,8]{1,0,4,3,2:T(8,128)(2,1)S(1)} %copy.33) | data formatting | bytes 524288 | tf_op jit(solution)/shard_map/reshape | solution.py:213
  71.2 1.1 %reshape_reshape.3 = bf16[1024,128]{0,1:T(8,128)(2,1)S(1)} reshape(bf16[32,32,2,8,8]{1,0,4,3,2:T(8,128)(2,1)S(1)} %copy.33) | data formatting | bytes 524288 | tf_op jit(solution)/shard_map/reshape;reshape | solution.py:215
  72.3 0.2 copy.40
  72.6 0.2 copy.39
  72.7 0.2 copy.37.rhs_ref
  72.9 0.0 copy-start.2
  72.9 0.9 %maximum_maximum_fusion.lhs_ref = bf16[2048,128]{1,0:T(8,128)(2,1)} fusion(bf16[1024,64]{1,0:T(8,128)(2,1)S(1)} %negate_bitcast_fusion, bf16[1024,64]{1,0:T(8,128)(2,1)S(1)} %bitcast.62, bf16[1024,128]{1,0:T(8,128)(2,1)S(1)} %copy.37.rhs_ref), kind=kLoop, calls=%fused_computation.2 | loop fusion | flops 1572864 | bytes 1048576 | tf_op jit(solution)/shard_map/concatenate | solution.py:216
  73.9 0.0 copy-done.2
  73.9 7.0 %shard_map.39 = f32[2048,1024]{1,0:T(8,128)} custom-call(bf16[2048,128]{1,0:T(8,128)(2,1)} %maximum_maximum_fusion.lhs_ref, bf16[1024,128]{1,0:T(8,128)(2,1)} %copy-done.2), custom_call_target="tpu_custom_call" | custom-call | tf_op jit(solution)/shard_map/pallas_call | solution.py:170
  (8 shorter events, 0.2 us)
Async XLA Ops:
  0.0 6.0 %copy-start.1 = (f32[8,8192]{1,0:T(8,128)S(1)}, f32[8,8192]{1,0:T(8,128)}, u32[]{:S(2)}) copy-start(f32[8,8192]{1,0:T(8,128)} %constant.81.clone.w_ref) | copy-start | bytes 786436
  0.0 6.0 %copy-start = (bf16[32,65536]{1,0:T(8,128)(2,1)S(1)}, bf16[32,65536]{1,0:T(8,128)(2,1)}, u32[]{:S(2)}) copy-start(bf16[32,65536]{1,0:T(8,128)(2,1)} %x_ref.3) | copy-start | bytes 12582916
  17.2 16.2 %copy-start.3 = (f32[2,32,256]{2,1,0:T(8,128)S(1)}, f32[2,32,256]{2,1,0:T(8,128)}, u32[]{:S(2)}) copy-start(f32[2,32,256]{2,1,0:T(8,128)} %param.6) | copy-start | bytes 196612
  17.2 16.5 %collective-permute-start = (f32[2,224,256]{2,1,0:T(8,128)S(1)}, f32[2,224,256]{2,1,0:T(8,128)S(1)}, u32[]{:S(2)}, u32[]{:S(2)}) collective-permute-start(f32[2,224,256]{2,1,0:T(8,128)S(1)} %shard_map.38), channel_id=1, source_target_pairs={{0,32},{32,64},{64,96},{96,128},{128,160},{160,192},{192,224},{1,3... | collective-permute-start | bytes 1376264 | tf_op jit(solution)/shard_map/ppermute | solution.py:20
  72.9 1.0 %copy-start.2 = (bf16[1024,128]{1,0:T(8,128)(2,1)}, bf16[1024,128]{1,0:T(8,128)(2,1)S(1)}, u32[]{:S(2)}) copy-start(bf16[1024,128]{1,0:T(8,128)(2,1)S(1)} %copy.37.rhs_ref) | copy-start | bytes 786436
